TPU v7x, 128 devices: a whole 4x4x4 slice. The times are simulated.
128 devices in a mesh: dp: 16 (over x, y), expert: 8 (over z, core).
Axes of the slice: x: 4, y: 4, z: 4, core: 2. Of those that a mesh axis runs over, the one named last changes fastest.
Arguments:
- frames: bfloat16 [65536, 1024], P(('dp', 'expert')), may hold values from -6 to 6
- lengths: int32 [256], P(('dp', 'expert')), may hold values from 64 to 256, as said below
- expert_ids: int32 [65536, 1], P(('dp', 'expert')), may hold values from 0 to 7; in each aligned block of 512 rows (0 to 511, 512 to 1023, ...) at most 72 rows name the same one
- conv_kernel: float32 [31, 1024], replicated, may hold values from -1 to 1
- conv_gain: float32 [1024], replicated, may hold values from 0.25 to 1.75
- ffn_gain: float32 [1024], replicated, may hold values from 0.25 to 1.75
- w_in: bfloat16 [8, 1024, 4096], P('expert'), may hold values from -0.1875 to 0.1875
- w_out: bfloat16 [8, 4096, 1024], P('expert'), may hold values from -0.09375 to 0.09375
- out_grad: bfloat16 [65536, 1024], P(('dp', 'expert')), may hold values from -6 to 6
Outputs:
- block_out: bfloat16 [65536, 1024], P(('dp', 'expert'))
- frames_grad: bfloat16 [65536, 1024], P(('dp', 'expert'))
- w_in_grad: float32 [8, 1024, 4096], P('expert', None, 'dp')
- w_out_grad: float32 [8, 4096, 1024], P('expert', 'dp')
- kernel_grad: float32 [31, 1024], replicated
- gain_grads: float32 [2, 1024], replicated
Inputs may be any that keep to these rules, and one draw needn't show every extreme that they name: `expert_ids`: in the rows of one device (aligned blocks of 512 rows) no expert is named more than 72 times, a bound that some block reaches. `lengths`: all utterances of some device have 256 live frames.
All inputs are finite; a program needn't handle non-finite values.
Results may differ from a plain program's by a relative error of at most 0.0053.
Values may be sent and summed in bfloat16 or wider, within the bound.
No kernel may reach another device: no remote copies, remote signals or barrier semaphores. Data moves between devices by JAX's collectives and lax.ppermute only.
A program may use at most 256 MiB of HBM per device.

v0:
```python
import jax
import jax.numpy as jnp
from jax import lax
from jax.sharding import PartitionSpec as P


def layer_norm(values, gain_vec):
    row_mean = jnp.mean(values, axis=-1, keepdims=True)
    centered = values - row_mean
    row_var = jnp.mean(centered * centered, axis=-1, keepdims=True)
    return centered * lax.rsqrt(row_var + 1e-05) * gain_vec


def conv_module(frames_f, live_mask, conv_kernel, conv_gain, ffn_gain):
    normed_conv = layer_norm(frames_f, conv_gain) * live_mask
    tap_count = conv_kernel.shape[0]
    half_span = (tap_count - 1) // 2
    utt_len = frames_f.shape[1]
    padded = jnp.pad(normed_conv, ((0, 0), (half_span, half_span), (0, 0)))
    conv_out = jnp.zeros_like(normed_conv)
    for tap_index in range(tap_count):
        conv_out = conv_out + conv_kernel[tap_index] * padded[:, tap_index : tap_index + utt_len]
    residual = frames_f + live_mask * jax.nn.silu(conv_out)
    return (residual, layer_norm(residual, ffn_gain))


def silu_slope(values):
    sig_val = jax.nn.sigmoid(values)
    return sig_val * (1.0 + values * (1.0 - sig_val))


def contract_rows(left_rows, right_rows):
    return lax.dot_general(
        left_rows, right_rows, (((0,), (0,)), ((), ())), preferred_element_type=jnp.float32
    )


def times_transpose(left_rows, matrix):
    return lax.dot_general(
        left_rows, matrix, (((1,), (1,)), ((), ())), preferred_element_type=jnp.float32
    )


def shards(frames, lengths, expert_ids, conv_kernel, conv_gain, ffn_gain, w_in, w_out, out_grad):
    utt_count = lengths.shape[0]
    frame_count = frames.shape[0]
    utt_len = frame_count // utt_count
    feat_width = frames.shape[1]
    expert_count = lax.axis_size("expert")
    capacity = max(8, 8 * (9 * frame_count // (64 * expert_count)))
    slot_total = expert_count * capacity
    live_mask = (jnp.arange(utt_len, dtype=jnp.int32)[None, :] < lengths[:, None]).astype(
        jnp.float32
    )[:, :, None]
    frames_f = frames.astype(jnp.float32).reshape(utt_count, utt_len, feat_width)
    residual, normed = conv_module(frames_f, live_mask, conv_kernel, conv_gain, ffn_gain)
    expert_in = normed.reshape(frame_count, feat_width).astype(jnp.bfloat16)
    live_flat = live_mask.reshape(frame_count) > 0.5
    target = jnp.where(live_flat, expert_ids[:, 0], expert_count)
    one_hot = (target[:, None] == jnp.arange(expert_count, dtype=jnp.int32)[None, :]).astype(
        jnp.int32
    )
    rank_in = jnp.sum((jnp.cumsum(one_hot, axis=0, dtype=jnp.int32) - 1) * one_hot, axis=1)
    dest_slot = jnp.where(live_flat, target * capacity + rank_in, slot_total)
    routed_grad = jnp.where(live_flat[:, None], out_grad, jnp.zeros_like(out_grad))
    send_in = (
        jnp.zeros((slot_total, feat_width), jnp.bfloat16).at[dest_slot].set(expert_in, mode="drop")
    )
    send_grad = (
        jnp.zeros((slot_total, feat_width), jnp.bfloat16)
        .at[dest_slot]
        .set(routed_grad, mode="drop")
    )
    recv_in, recv_grad = (
        lax.all_to_all(
            send_in.reshape(expert_count, capacity, feat_width),
            "expert",
            split_axis=0,
            concat_axis=0,
            tiled=True,
        ),
        lax.all_to_all(
            send_grad.reshape(expert_count, capacity, feat_width),
            "expert",
            split_axis=0,
            concat_axis=0,
            tiled=True,
        ),
    )
    routed_in = recv_in.reshape(slot_total, feat_width)
    grad_rows = recv_grad.reshape(slot_total, feat_width)
    weights_in = w_in[0]
    weights_out = w_out[0]
    pre_act = jnp.dot(routed_in, weights_in, preferred_element_type=jnp.float32)
    hidden = jax.nn.silu(pre_act).astype(jnp.bfloat16)
    out_rows = jnp.dot(hidden, weights_out, preferred_element_type=jnp.float32).astype(jnp.bfloat16)
    hidden_grad = times_transpose(grad_rows, weights_out)
    pre_grad = (hidden_grad * silu_slope(pre_act)).astype(jnp.bfloat16)
    back_rows = times_transpose(pre_grad, weights_in).astype(jnp.bfloat16)
    ret_out, ret_back = (
        lax.all_to_all(
            out_rows.reshape(expert_count, capacity, feat_width),
            "expert",
            split_axis=0,
            concat_axis=0,
            tiled=True,
        ),
        lax.all_to_all(
            back_rows.reshape(expert_count, capacity, feat_width),
            "expert",
            split_axis=0,
            concat_axis=0,
            tiled=True,
        ),
    )
    full_in = contract_rows(routed_in, pre_grad)
    full_out = contract_rows(hidden, grad_rows)
    grad_in, grad_out = (
        lax.psum_scatter(full_in, "dp", scatter_dimension=1, tiled=True),
        lax.psum_scatter(full_out, "dp", scatter_dimension=0, tiled=True),
    )
    safe_slot = jnp.minimum(dest_slot, slot_total - 1)
    zero_rows = jnp.zeros((frame_count, feat_width), jnp.float32)
    expert_out = jnp.where(
        live_flat[:, None],
        ret_out.reshape(slot_total, feat_width)[safe_slot].astype(jnp.float32),
        zero_rows,
    )
    expert_back = jnp.where(
        live_flat[:, None],
        ret_back.reshape(slot_total, feat_width)[safe_slot].astype(jnp.float32),
        zero_rows,
    )
    block_out = (residual.reshape(frame_count, feat_width) + expert_out).astype(jnp.bfloat16)

    def local_map(frames_in, kernel_in, gain_conv, gain_ffn):
        return conv_module(frames_in, live_mask, kernel_in, gain_conv, gain_ffn)

    unused_out, pull_back = jax.vjp(local_map, frames_f, conv_kernel, conv_gain, ffn_gain)
    frames_part, kernel_part, conv_part, ffn_part = pull_back(
        (
            out_grad.astype(jnp.float32).reshape(utt_count, utt_len, feat_width),
            expert_back.reshape(utt_count, utt_len, feat_width),
        )
    )
    kernel_grad, gain_grads = lax.psum(
        (kernel_part, jnp.stack([conv_part, ffn_part])), ("dp", "expert")
    )
    frames_grad = frames_part.reshape(frame_count, feat_width).astype(jnp.bfloat16)
    return (block_out, frames_grad, grad_in[None], grad_out[None], kernel_grad, gain_grads)


def solution(mesh):
    return jax.shard_map(
        shards,
        mesh=mesh,
        in_specs=(
            P(("dp", "expert"), None),
            P(("dp", "expert")),
            P(("dp", "expert"), None),
            P(),
            P(),
            P(),
            P("expert", None, None),
            P("expert", None, None),
            P(("dp", "expert"), None),
        ),
        out_specs=(
            P(("dp", "expert"), None),
            P(("dp", "expert"), None),
            P("expert", None, "dp"),
            P("expert", "dp", None),
            P(),
            P(),
        ),
        check_vma=False,
    )
```

profile of v0, /device:TPU:1, one launch (start us, length us, event | category | flops | bytes accessed | tf_op | source)
XLA Modules:
  0.0 402.6 jit_solution(15675483009608328788)
XLA Ops:
  8.1 1.5 convert_reduce_fusion
  9.6 1.6 multiply_reduce_fusion.34
  11.4 0.6 copy-done.19
  12.1 1.1 reduce-window.6
  13.2 0.2 slice_reduce_fusion
  13.5 0.1 fusion.35
  13.6 0.4 multiply_multiply_fusion
  14.1 9.6 %multiply_add_fusion = (f32[2,256,1024]{2,1,0:T(8,128)S(1)}, f32[2,256,1024]{2,1,0:T(8,128)}) fusion(f32[2,256]{1,0:T(2,128)S(1)} %get-tuple-element.113, bf16[512,1024]{1,0:T(8,128)(2,1)S(1)} %copy-done, f32[1024]{0:T(1024)S(1)} %bitcast.198, f32[1024]{0:T(1024)S(1)} %bitcast.152, f32[1024]{0:T(1024)S(1)} %bitcast.154, f32[1024]{0:T(1024)S(1)} %bitcast.156, ...), kind=kLoop, calls=%fused_computation.105 | loop fusion | flops 35651584 | bytes 7469056 | tf_op jit(solution)/shard_map/add | solution.py:23
  23.7 0.2 reduce_sum.378
  23.9 0.4 multiply_reduce_fusion.33
  24.2 0.1 copy-done.18
  24.4 1.3 multiply_convert_fusion.2
  25.7 4.4 %scatter_custom_fusion = bf16[576,1024]{1,0:T(8,128)(2,1)} fusion(s32[512]{0:T(512)S(1)} %bitcast.253, bf16[512,1024]{1,0:T(8,128)(2,1)} %bitcast.151, bf16[]{:T(256)} %constant.44.clone.1), kind=kCustom, calls=%fused_computation.148 | custom fusion | bytes 1180160 | tf_op jit(solution)/shard_map/scatter | solution.py:67
  30.0 6.8 %all-to-all-start = ((bf16[8,72,1024]{2,1,0:T(8,128)(2,1)}), bf16[8,72,1024]{2,1,0:T(8,128)(2,1)}, u32[]{:S(2)}, u32[]{:S(2)}) async-start(bf16[8,72,1024]{2,1,0:T(8,128)(2,1)} %bitcast.145), calls=%async_computation | async-start | bytes 2359296 | tf_op jit(solution)/shard_map/all_to_all | solution.py:75
  36.9 3.7 scatter_custom_fusion.1
  40.6 12.7 %all-to-all-done = bf16[8,72,1024]{2,1,0:T(8,128)(2,1)} async-done(((bf16[8,72,1024]{2,1,0:T(8,128)(2,1)}), bf16[8,72,1024]{2,1,0:T(8,128)(2,1)}, u32[]{:S(2)}, u32[]{:S(2)}) %all-to-all-start) | async-done | bytes 1179680 | tf_op jit(solution)/shard_map/all_to_all | solution.py:75
  53.3 5.0 %all-to-all-start.2 = ((bf16[8,72,1024]{2,1,0:T(8,128)(2,1)}), bf16[8,72,1024]{2,1,0:T(8,128)(2,1)S(1)}, u32[]{:S(2)}, u32[]{:S(2)}) async-start(bf16[8,72,1024]{2,1,0:T(8,128)(2,1)} %bitcast.144), calls=%async_computation.2 | async-start | bytes 2359296 | tf_op jit(solution)/shard_map/all_to_all | solution.py:82
  58.3 9.9 %fusion.6 = f32[576,4096]{1,0:T(8,128)} fusion(bf16[576,1024]{1,0:T(8,128)(2,1)} %bitcast.41, bf16[1,1024,4096]{2,1,0:T(8,128)(2,1)} %param.15), kind=kOutput, calls=%fused_computation.13 | convolution fusion | flops 4831838208 | bytes 19005440 | tf_op jit(solution)/shard_map/dot_general | solution.py:94
  68.2 6.5 %all-to-all-done.2 = bf16[8,72,1024]{2,1,0:T(8,128)(2,1)S(1)} async-done(((bf16[8,72,1024]{2,1,0:T(8,128)(2,1)}), bf16[8,72,1024]{2,1,0:T(8,128)(2,1)S(1)}, u32[]{:S(2)}, u32[]{:S(2)}) %all-to-all-start.2) | async-done | bytes 1179680 | tf_op jit(solution)/shard_map/all_to_all | solution.py:82
  74.7 11.2 %multiply_convert_fusion = bf16[576,4096]{1,0:T(8,128)(2,1)S(1)} fusion(f32[576,4096]{1,0:T(8,128)} %fusion.6, bf16[576,1024]{1,0:T(8,128)(2,1)S(1)} %bitcast.146, bf16[1,4096,1024]{2,1,0:T(8,128)(2,1)} %param.16), kind=kOutput, calls=%fused_computation.4 | convolution fusion | flops 4853071872 | bytes 23724032 | tf_op jit(solution)/shard_map/dot_general | solution.py:39
  85.9 10.4 %fusion.21 = bf16[576,1024]{1,0:T(8,128)(2,1)} fusion(bf16[576,4096]{1,0:T(8,128)(2,1)S(1)} %multiply_convert_fusion, bf16[1,1024,4096]{2,1,0:T(8,128)(2,1)} %param.15), kind=kOutput, calls=%fused_computation.110 | convolution fusion | flops 4832428032 | bytes 14286848 | tf_op jit(solution)/shard_map/dot_general | solution.py:39
  96.3 4.4 %all-to-all-start.3 = ((bf16[8,72,1024]{2,1,0:T(8,128)(2,1)}), bf16[8,72,1024]{2,1,0:T(8,128)(2,1)S(1)}, u32[]{:S(2)}, u32[]{:S(2)}) async-start(bf16[8,72,1024]{2,1,0:T(8,128)(2,1)} %bitcast.148), calls=%async_computation.3 | async-start | bytes 2359296 | tf_op jit(solution)/shard_map/all_to_all | solution.py:108
  100.8 0.2 all-reduce.65.cloned.1.call-start
  100.9 16.2 %all-to-all-done.3 = bf16[8,72,1024]{2,1,0:T(8,128)(2,1)S(1)} async-done(((bf16[8,72,1024]{2,1,0:T(8,128)(2,1)}), bf16[8,72,1024]{2,1,0:T(8,128)(2,1)S(1)}, u32[]{:S(2)}, u32[]{:S(2)}) %all-to-all-start.3) | async-done | bytes 1179680 | tf_op jit(solution)/shard_map/all_to_all | solution.py:108
  117.2 2.8 gather_fusion.1
  120.0 2.6 fusion.16
  122.6 1.9 add_add_fusion.1
  124.6 1.9 reduce_sum.384
  126.5 20.3 %multiply_reduce_fusion.30 = (f32[1024]{0:T(1024)S(1)}, f32[1024]{0:T(1024)S(1)}, f32[1024]{0:T(1024)S(1)}, f32[1024]{0:T(1024)S(1)}, f32[1024]{0:T(1024)S(1)}, ...) fusion(f32[2,256,1024]{2,1,0:T(8,128)} %copy-done.5, ...), kind=kLoop, calls=%fused_computation.99 | loop fusion | flops 27249664 | bytes 11610624 | tf_op jit(solution)/shard_map/transpose(jvp())/reduce_sum | solution.py:22
  146.8 4.9 %multiply_reduce_fusion.31 = (f32[1024]{0:T(1024)S(1)}, f32[1024]{0:T(1024)S(1)}, f32[1024]{0:T(1024)S(1)}, f32[1024]{0:T(1024)S(1)}, f32[1024]{0:T(1024)S(1)}, ...) fusion(f32[2,256,1024]{2,1,0:T(8,128)S(1)} %get-tuple-element.4, ...), kind=kLoop, calls=%fused_computation.100 | loop fusion | flops 18855936 | bytes 4268032 | tf_op jit(solution)/shard_map/transpose(jvp())/reduce_sum | solution.py:22
  151.8 0.9 pad_add_fusion.7
  152.7 0.3 reduce-scatter.5.cloned.1.call-start
  152.9 14.5 %fusion.39 = f32[4096,1024]{1,0:T(8,128)} fusion(bf16[576,1024]{1,0:T(8,128)(2,1)S(1)} %bitcast.147, f32[576,4096]{1,0:T(8,128)} %fusion.6), kind=kOutput, calls=%fused_computation.177 | convolution fusion | flops 4843634688 | bytes 27394048 | tf_op jit(solution)/shard_map/dot_general | solution.py:33
  167.5 12.2 %fusion.44 = f32[1024,4096]{1,0:T(8,128)} fusion(bf16[576,1024]{1,0:T(8,128)(2,1)} %bitcast.41, bf16[576,4096]{1,0:T(8,128)(2,1)} %copy-done.13), kind=kOutput, calls=%fused_computation.180 | convolution fusion | flops 4831838208 | bytes 22675456 | tf_op jit(solution)/shard_map/dot_general | solution.py:33
  179.7 10.3 %fusion.24 = bf16[576,1024]{1,0:T(8,128)(2,1)S(1)} fusion(bf16[1,4096,1024]{2,1,0:T(8,128)(2,1)} %param.16, f32[576,4096]{1,0:T(8,128)} %fusion.6), kind=kOutput, calls=%fused_computation.111 | convolution fusion | flops 4844224512 | bytes 19005440 | tf_op jit(solution)/shard_map/dot_general | solution.py:96
  190.1 20.3 %all_to_all.20 = bf16[8,72,1024]{2,1,0:T(8,128)(2,1)S(1)} all-to-all(bf16[8,72,1024]{2,1,0:T(8,128)(2,1)S(1)} %bitcast.149), channel_id=1, replica_groups=mesh['dp'=16,'expert'=8] {'expert'}, dimensions={0} | all-to-all | bytes 2359296 | tf_op jit(solution)/shard_map/all_to_all | solution.py:101
  210.4 2.8 gather_fusion
  213.1 10.8 %broadcast_multiply_fusion.1 = (f32[2,256,1024]{2,1,0:T(8,128)}, f32[2,256,1024]{2,1,0:T(8,128)}, f32[2,256,1024]{2,1,0:T(8,128)}, f32[2,256,1024]{2,1,0:T(8,128...) fusion(f32[2,256,1024]{2,1,0:T(8,128)} %copy-done.7, ...), kind=kLoop, calls=%fused_computation.115 | loop fusion | flops 6815744 | bytes 29413376 | tf_op jit(solution)/shard_map/transpose(jvp())/mul | solution.py:22
  223.9 13.4 %broadcast_multiply_fusion = (f32[2,256,1024]{2,1,0:T(8,128)}, f32[2,256,1024]{2,1,0:T(8,128)}, f32[2,256,1024]{2,1,0:T(8,128)}, f32[2,256,1024]{2,1,0:T(8,128)}...) fusion(f32[2,256,1024]{2,1,0:T(8,128)S(1)} %copy-done.8, ...), kind=kLoop, calls=%fused_computation.114 | loop fusion | flops 9437184 | bytes 39919616 | tf_op jit(solution)/shard_map/transpose(jvp())/mul | solution.py:22
  237.3 21.8 %pad_add_fusion = f32[2,286,1024]{2,1,0:T(8,128)} fusion(f32[2,256,1024]{2,1,0:T(8,128)} %get-tuple-element.56, f32[2,256,1024]{2,1,0:T(8,128)} %get-tuple-element.57, f32[2,256,1024]{2,1,0:T(8,128)} %get-tuple-element.58, f32[2,256,1024]{2,1,0:T(8,128)} %get-tuple-element.59, f32[2,256,1024]{2,1,0:T(8,128)} %get-tuple-element.60, ...), kind=kLoop, calls=%fused_computation.18 | loop fusion | flops 14057472 | bytes 54771712 | tf_op jit(solution)/shard_map/transpose(jvp())/add_any | solution.py:22
  259.2 6.3 %multiply_reduce_fusion.32 = (f32[2,256]{1,0:T(2,128)S(1)}, f32[2,256,1024]{2,1,0:T(8,128)S(1)}, f32[2,256,1024]{2,1,0:T(8,128)S(1)}) fusion(f32[1024]{0:T(1024)S(1)} %copy-done.17, f32[2,256]{1,0:T(2,128)S(1)} %div.54, bf16[2,256,1024]{2,1,0:T(8,128)(2,1)S(1)} %bitcast.142, f32[2,256]{1,0:T(2,128)S(1)} %get-tuple-element.113, ...), kind=kLoop, calls=%fused_computation.102 | loop fusion | flops 6290944 | bytes 19933184 | tf_op jit(solution)/shard_map/transpose(jvp())/reduce_sum | solution.py:11
  265.5 1.1 multiply_reduce_fusion
  266.6 0.2 copy-done.9
  266.8 67.7 %psum.15 = f32[2,1024]{1,0:T(2,128)} all-reduce(f32[2,1024]{1,0:T(2,128)S(1)} %pad_maximum_fusion), channel_id=1, replica_groups=mesh['dp'=16,'expert'=8] {'dp','expert'}, use_global_device_ids=true, to_apply=%region_49.50 | all-reduce | flops 2048 | bytes 16384 | tf_op jit(solution)/shard_map/psum | solution.py:146
  334.5 3.0 fusion.18
  337.5 2.4 add_convert_fusion
  339.9 53.1 %reduce-scatter.3.cloned.1.call-done = f32[1024,256]{1,0:T(8,128)} async-done(((f32[1024,4096]{1,0:T(8,128)}), f32[1024,256]{1,0:T(8,128)}) %reduce-scatter.3.cloned.1.call-update) | async-done | bytes 1048592 | tf_op jit(solution)/shard_map/reduce_scatter | solution.py:119
  393.1 1.6 copy.17
  (77 shorter events, 0.6 us)
Async XLA Ops:
  8.0 5.6 %copy-start = (bf16[512,1024]{1,0:T(8,128)(2,1)S(1)}, bf16[512,1024]{1,0:T(8,128)(2,1)}, u32[]{:S(2)}) copy-start(bf16[512,1024]{1,0:T(8,128)(2,1)} %param.9) | copy-start | bytes 3145732
  8.0 3.2 copy-start.16
  8.0 3.9 copy-start.24
  8.0 4.0 copy-start.21
  8.0 5.6 %copy-start.17 = (f32[1024]{0:T(1024)S(1)}, f32[1024]{0:T(1024)}, u32[]{:S(2)}) copy-start(f32[1024]{0:T(1024)} %param.13) | copy-start | bytes 12292
  11.4 0.6 copy-start.19
  14.1 9.6 %copy-start.5 = (f32[2,256,1024]{2,1,0:T(8,128)}, f32[2,256,1024]{2,1,0:T(8,128)S(1)}, u32[]{:S(2)}) copy-start(f32[2,256,1024]{2,1,0:T(8,128)S(1)} %multiply_multiply_fusion) | copy-start | bytes 6291460
  23.7 0.7 copy-start.18
  25.7 11.2 %copy-start.11 = (bf16[512,1024]{1,0:T(8,128)(2,1)S(1)}, bf16[512,1024]{1,0:T(8,128)(2,1)}, u32[]{:S(2)}) copy-start(bf16[512,1024]{1,0:T(8,128)(2,1)} %param.17) | copy-start | bytes 3145732
  30.0 23.3 %all-to-all-start = ((bf16[8,72,1024]{2,1,0:T(8,128)(2,1)}), bf16[8,72,1024]{2,1,0:T(8,128)(2,1)}, u32[]{:S(2)}, u32[]{:S(2)}) async-start(bf16[8,72,1024]{2,1,0:T(8,128)(2,1)} %bitcast.145), calls=%async_computation | async-start | bytes 2359296 | tf_op jit(solution)/shard_map/all_to_all | solution.py:75
  36.9 16.5 %copy-start.22 = (pred[512]{0:T(512)(128)(4,1)}, pred[512]{0:T(512)(128)(4,1)S(1)}, u32[]{:S(2)}) copy-start(pred[512]{0:T(512)(128)(4,1)S(1)} %gt.26) | copy-start | bytes 1540
  53.3 21.4 %all-to-all-start.2 = ((bf16[8,72,1024]{2,1,0:T(8,128)(2,1)}), bf16[8,72,1024]{2,1,0:T(8,128)(2,1)S(1)}, u32[]{:S(2)}, u32[]{:S(2)}) async-start(bf16[8,72,1024]{2,1,0:T(8,128)(2,1)} %bitcast.144), calls=%async_computation.2 | async-start | bytes 2359296 | tf_op jit(solution)/shard_map/all_to_all | solution.py:82
  74.7 11.2 %copy-start.14 = (bf16[8,72,1024]{2,1,0:T(8,128)(2,1)}, bf16[8,72,1024]{2,1,0:T(8,128)(2,1)S(1)}, u32[]{:S(2)}) copy-start(bf16[8,72,1024]{2,1,0:T(8,128)(2,1)S(1)} %all-to-all-done.2) | copy-start | bytes 3538948
  85.9 10.4 %copy-start.13 = (bf16[576,4096]{1,0:T(8,128)(2,1)}, bf16[576,4096]{1,0:T(8,128)(2,1)S(1)}, u32[]{:S(2)}) copy-start(bf16[576,4096]{1,0:T(8,128)(2,1)S(1)} %multiply_convert_fusion) | copy-start | bytes 14155780
  96.3 20.8 %all-to-all-start.3 = ((bf16[8,72,1024]{2,1,0:T(8,128)(2,1)}), bf16[8,72,1024]{2,1,0:T(8,128)(2,1)S(1)}, u32[]{:S(2)}, u32[]{:S(2)}) async-start(bf16[8,72,1024]{2,1,0:T(8,128)(2,1)} %bitcast.148), calls=%async_computation.3 | async-start | bytes 2359296 | tf_op jit(solution)/shard_map/all_to_all | solution.py:108
  100.8 239.2 %all-reduce.65.cloned.1.call-start = ((), (), s32[]{:S(2)}) async-start(), calls=%async_computation.8 | async-start | bytes 262144 | tf_op jit(solution)/shard_map/psum | solution.py:146
  120.0 2.7 copy-start.3
  124.6 1.9 copy-start.1
  126.5 20.4 %copy-start.6 = (f32[2,256,1024]{2,1,0:T(8,128)S(1)}, f32[2,256,1024]{2,1,0:T(8,128)}, u32[]{:S(2)}) copy-start(f32[2,256,1024]{2,1,0:T(8,128)} %copy-done.5) | copy-start | bytes 6291460
  146.8 4.9 %copy-start.7 = (f32[2,256,1024]{2,1,0:T(8,128)}, f32[2,256,1024]{2,1,0:T(8,128)S(1)}, u32[]{:S(2)}) copy-start(f32[2,256,1024]{2,1,0:T(8,128)S(1)} %get-tuple-element.41) | copy-start | bytes 6291460
  146.8 6.1 %copy-start.15 = (bf16[8,72,1024]{2,1,0:T(8,128)(2,1)S(1)}, bf16[8,72,1024]{2,1,0:T(8,128)(2,1)}, u32[]{:S(2)}) copy-start(bf16[8,72,1024]{2,1,0:T(8,128)(2,1)} %copy-done.14) | copy-start | bytes 3538948
  152.7 187.3 %reduce-scatter.5.cloned.1.call-start = ((), (), s32[]{:S(2)}) async-start(), calls=%async_computation.7 | async-start | bytes 17825792 | tf_op jit(solution)/shard_map/reduce_scatter | solution.py:120
  167.5 225.6 %reduce-scatter.3.cloned.1.call-start = ((), (), s32[]{:S(2)}) async-start(), calls=%async_computation.6 | async-start | bytes 17825792 | tf_op jit(solution)/shard_map/reduce_scatter | solution.py:119
  213.1 10.8 %copy-start.8 = (f32[2,256,1024]{2,1,0:T(8,128)S(1)}, f32[2,256,1024]{2,1,0:T(8,128)}, u32[]{:S(2)}) copy-start(f32[2,256,1024]{2,1,0:T(8,128)} %copy-done.7) | copy-start | bytes 6291460
  237.3 21.8 %copy-start.2 = (bf16[512,1024]{1,0:T(8,128)(2,1)S(1)}, bf16[512,1024]{1,0:T(8,128)(2,1)}, u32[]{:S(2)}) copy-start(bf16[512,1024]{1,0:T(8,128)(2,1)} %param.9) | copy-start | bytes 3145732
  259.1 6.4 %copy-start.20 = (f32[2,256]{1,0:T(2,128)S(1)}, f32[2,256]{1,0:T(2,128)}, u32[]{:S(2)}) copy-start(f32[2,256]{1,0:T(2,128)} %copy-done.19) | copy-start | bytes 6148
  265.5 1.3 copy-start.9
  265.5 69.0 %copy-start.23 = (pred[512]{0:T(512)(128)(4,1)S(1)}, pred[512]{0:T(512)(128)(4,1)}, u32[]{:S(2)}) copy-start(pred[512]{0:T(512)(128)(4,1)} %copy-done.22) | copy-start | bytes 1540
  334.5 3.0 copy-start.4
  334.5 3.0 copy-start.10
  334.5 3.0 copy-start.12
Sparse Core Ops, SparseCore 0:
  152.8 172.7 all-reduce.64
Sparse Core Ops, SparseCore 1:
  167.5 110.5 reduce-scatter.4
  282.0 111.0 reduce-scatter.2
where the time goes:
time: 410 us; the launch traced here: 403 us
  other arithmetic  112 us (27%)
  waiting for transfers between devices  88.6 us (22%)
  blocking collectives  88 us (21%)
  matrix products  68.5 us (17%)
  starting transfers between devices  16.7 us (4%)
  between operations  16.4 us (4%)
  local copies, waits for them, and re-layouts  12.9 us (3%)
    psum x1, blocking collectives, shards(): lax.psum((kernel_part, jnp.stack([conv_part, ffn_part])), ('dp', 'expert'))  67.7 us
    reduce_scatter x1, waiting for transfers between devices, shards(): lax.psum_scatter(full_in, 'dp', scatter_dimension=1, tiled=True)  53.1 us
    dot_general x2, matrix products, contract_rows(): lax.dot_general(left_rows, right_rows, (((0,), (0,)), ((), ())), preferre...  26.7 us
    reduce_sum x2, other arithmetic, conv_module(): conv_kernel[tap_index] * padded[:, tap_index:tap_index + utt_len]  25.2 us
    mul x2, other arithmetic, conv_module(): conv_kernel[tap_index] * padded[:, tap_index:tap_index + utt_len]  24.2 us
    add_any x1, other arithmetic, conv_module(): padded[:, tap_index:tap_index + utt_len]  21.8 us
    dot_general x2, matrix products, times_transpose(): lax.dot_general(left_rows, matrix, (((1,), (1,)), ((), ())), preferred_el...  21.6 us
    all_to_all x1, blocking collectives, shards(): lax.all_to_all(out_rows.reshape(expert_count, capacity, feat_width), 'exp...  20.3 us
  transfers between devices with their start and end apart: 6, of which 4 were waited for; matrix products, arithmetic and copies ran while one was open for 28% of the time, Pallas kernels for 0%

commit v1 on v0

--- a/solution.py
+++ b/solution.py
@@ -39,6 +39,17 @@
     return lax.dot_general(
         left_rows, matrix, (((1,), (1,)), ((), ())), preferred_element_type=jnp.float32
     )
+
+
+def butterfly_sum(values, axis_names):
+    for axis_name in axis_names:
+        axis_len = lax.axis_size(axis_name)
+        step = 1
+        while step < axis_len:
+            pairs = [(i, i ^ step) for i in range(axis_len)]
+            values = values + lax.ppermute(values, axis_name, pairs)
+            step *= 2
+    return values
 
 
 def shards(frames, lengths, expert_ids, conv_kernel, conv_gain, ffn_gain, w_in, w_out, out_grad):
@@ -93,9 +104,17 @@
     weights_out = w_out[0]
     pre_act = jnp.dot(routed_in, weights_in, preferred_element_type=jnp.float32)
     hidden = jax.nn.silu(pre_act).astype(jnp.bfloat16)
+    full_out = contract_rows(hidden, grad_rows)
+    full_out, pre_act, hidden, grad_rows, routed_in = lax.optimization_barrier(
+        (full_out, pre_act, hidden, grad_rows, routed_in)
+    )
+    grad_out = lax.psum_scatter(full_out, "dp", scatter_dimension=0, tiled=True)
     out_rows = jnp.dot(hidden, weights_out, preferred_element_type=jnp.float32).astype(jnp.bfloat16)
     hidden_grad = times_transpose(grad_rows, weights_out)
     pre_grad = (hidden_grad * silu_slope(pre_act)).astype(jnp.bfloat16)
+    full_in = contract_rows(routed_in, pre_grad)
+    full_in, out_rows, pre_grad = lax.optimization_barrier((full_in, out_rows, pre_grad))
+    grad_in = lax.psum_scatter(full_in, "dp", scatter_dimension=1, tiled=True)
     back_rows = times_transpose(pre_grad, weights_in).astype(jnp.bfloat16)
     ret_out, ret_back = (
         lax.all_to_all(
@@ -112,12 +131,6 @@
             concat_axis=0,
             tiled=True,
         ),
-    )
-    full_in = contract_rows(routed_in, pre_grad)
-    full_out = contract_rows(hidden, grad_rows)
-    grad_in, grad_out = (
-        lax.psum_scatter(full_in, "dp", scatter_dimension=1, tiled=True),
-        lax.psum_scatter(full_out, "dp", scatter_dimension=0, tiled=True),
     )
     safe_slot = jnp.minimum(dest_slot, slot_total - 1)
     zero_rows = jnp.zeros((frame_count, feat_width), jnp.float32)
@@ -143,9 +156,12 @@
             expert_back.reshape(utt_count, utt_len, feat_width),
         )
     )
-    kernel_grad, gain_grads = lax.psum(
-        (kernel_part, jnp.stack([conv_part, ffn_part])), ("dp", "expert")
+    tap_count = kernel_part.shape[0]
+    small_grads = butterfly_sum(
+        jnp.concatenate([kernel_part, conv_part[None], ffn_part[None]], axis=0), ("dp", "expert")
     )
+    kernel_grad = small_grads[:tap_count]
+    gain_grads = small_grads[tap_count:]
     frames_grad = frames_part.reshape(frame_count, feat_width).astype(jnp.bfloat16)
     return (block_out, frames_grad, grad_in[None], grad_out[None], kernel_grad, gain_grads)
 

time: 410 us -> 340 us (0.83)
  blocking collectives: 88 us -> 0 us
  starting transfers between devices: 16.7 us -> 49.1 us
  waiting for transfers between devices: 88.6 us -> 78.9 us
    psum x1 -> x0, blocking collectives: 67.7 us -> none  [shards(): lax.psum((kernel_part, jnp.stack([conv_part, ffn_part])), ('dp', 'expert'))]
    reduce_scatter x2, waiting for transfers between devices: 53.1 us -> 23.2 us  [the longest x1 23.2 us: shards(): grad_in = lax.psum_scatter(full_in, 'dp', scatter_dimension=1, tiled=True)]
    ppermute x0 -> x7, waiting for transfers between devices: none -> 26.6 us  [butterfly_sum(): values = values + lax.ppermute(values, axis_name, pairs)]
    all_to_all x1 -> x0, blocking collectives: 20.3 us -> none  [shards(): lax.all_to_all(out_rows.reshape(expert_count, capacity, feat_width), 'exp...]
    ppermute x0 -> x7, starting transfers between devices: none -> 15.9 us  [butterfly_sum(): values = values + lax.ppermute(values, axis_name, pairs)]
    reduce_scatter x2, starting transfers between devices: 0.3 us -> 10.8 us  [the longest x1 10.8 us: shards(): grad_out = lax.psum_scatter(full_out, 'dp', scatter_dimension=0, tiled=True)]
    all_to_all x1, waiting for transfers between devices: 6.47 us -> 0.01 us  [shards(): lax.all_to_all(send_grad.reshape(expert_count, capacity, feat_width), 'ex...]
    all_to_all x0 -> x1, starting transfers between devices: none -> 6.03 us  [shards(): lax.all_to_all(out_rows.reshape(expert_count, capacity, feat_width), 'exp...]
  transfers between devices with their start and end apart: 6 -> 13, of which waited for: 4 -> 8; matrix products, arithmetic and copies ran while one was open for 28% -> 47% of each run, Pallas kernels for 0% -> 0%
where the time goes in v1:
time: 340 us; the launch traced here: 336 us
  other arithmetic  113 us (33%)
  waiting for transfers between devices  78.9 us (23%)
  matrix products  66.3 us (20%)
  starting transfers between devices  49.1 us (14%)
  between operations  14.6 us (4%)
  local copies, waits for them, and re-layouts  14.1 us (4%)
    ppermute x7, waiting for transfers between devices, butterfly_sum(): values = values + lax.ppermute(values, axis_name, pairs)  26.6 us
    reduce_sum x2, other arithmetic, conv_module(): conv_kernel[tap_index] * padded[:, tap_index:tap_index + utt_len]  25.2 us
    dot_general x2, matrix products, contract_rows(): lax.dot_general(left_rows, right_rows, (((0,), (0,)), ((), ())), preferre...  24.1 us
    reduce_scatter x1, waiting for transfers between devices, shards(): grad_in = lax.psum_scatter(full_in, 'dp', scatter_dimension=1, tiled=True)  23.2 us
    add_any x1, other arithmetic, conv_module(): padded[:, tap_index:tap_index + utt_len]  22.6 us
    mul x2, other arithmetic, conv_module(): conv_kernel[tap_index] * padded[:, tap_index:tap_index + utt_len]  21.6 us
    dot_general x2, matrix products, times_transpose(): lax.dot_general(left_rows, matrix, (((1,), (1,)), ((), ())), preferred_el...  20.7 us
    all_to_all x1, waiting for transfers between devices, shards(): lax.all_to_all(back_rows.reshape(expert_count, capacity, feat_width), 'ex...  16.3 us
  transfers between devices with their start and end apart: 13, of which 8 were waited for; matrix products, arithmetic and copies ran while one was open for 47% of the time, Pallas kernels for 0%

profile of v1, /device:TPU:1, one launch (start us, length us, event | category | flops | bytes accessed | tf_op | source)
XLA Modules:
  0.0 336.1 jit_solution(4848940986483531254)
XLA Ops:
  7.2 1.5 convert_reduce_fusion
  8.8 1.6 multiply_reduce_fusion.34
  10.7 1.1 reduce-window.6
  12.7 9.6 %multiply_add_fusion = (f32[2,256,1024]{2,1,0:T(8,128)S(1)}, f32[2,256,1024]{2,1,0:T(8,128)}) fusion(f32[2,256]{1,0:T(2,128)S(1)} %get-tuple-element.129, bf16[512,1024]{1,0:T(8,128)(2,1)S(1)} %copy-done, f32[1024]{0:T(1024)S(1)} %bitcast.206, f32[1024]{0:T(1024)S(1)} %bitcast.160, f32[1024]{0:T(1024)S(1)} %bitcast.162, f32[1024]{0:T(1024)S(1)} %bitcast.164, ...), kind=kLoop, calls=%fused_computation.104 | loop fusion | flops 35651584 | bytes 7469056 | tf_op jit(solution)/shard_map/add | solution.py:23
  23.0 1.3 multiply_convert_fusion.2
  24.3 4.4 %scatter_custom_fusion = bf16[576,1024]{1,0:T(8,128)(2,1)} fusion(s32[512]{0:T(512)S(1)} %bitcast.259, bf16[512,1024]{1,0:T(8,128)(2,1)} %bitcast.155, bf16[]{:T(256)} %constant.44.clone.1), kind=kCustom, calls=%fused_computation.147 | custom fusion | bytes 1180160 | tf_op jit(solution)/shard_map/scatter | solution.py:78
  28.6 6.8 %all-to-all-start = ((bf16[8,72,1024]{2,1,0:T(8,128)(2,1)}), bf16[8,72,1024]{2,1,0:T(8,128)(2,1)}, u32[]{:S(2)}, u32[]{:S(2)}) async-start(bf16[8,72,1024]{2,1,0:T(8,128)(2,1)} %bitcast.149), calls=%async_computation | async-start | bytes 2359296 | tf_op jit(solution)/shard_map/all_to_all | solution.py:86
  35.5 3.7 %scatter_custom_fusion.1 = bf16[576,1024]{1,0:T(8,128)(2,1)} fusion(s32[512]{0:T(512)S(1)} %bitcast.260, bf16[512,1024]{1,0:T(8,128)(2,1)S(1)} %copy-done.7, pred[512]{0:T(512)(128)(4,1)S(1)} %gt.26, bf16[]{:T(256)} %constant.44.clone.1), kind=kCustom, calls=%fused_computation.111 | custom fusion | flops 524288 | bytes 2229760 | tf_op jit(solution)/shard_map/scatter | solution.py:83
  39.2 12.7 %all-to-all-done = bf16[8,72,1024]{2,1,0:T(8,128)(2,1)} async-done(((bf16[8,72,1024]{2,1,0:T(8,128)(2,1)}), bf16[8,72,1024]{2,1,0:T(8,128)(2,1)}, u32[]{:S(2)}, u32[]{:S(2)}) %all-to-all-start) | async-done | bytes 1179680 | tf_op jit(solution)/shard_map/all_to_all | solution.py:86
  51.9 4.4 %all-to-all-start.1 = ((bf16[8,72,1024]{2,1,0:T(8,128)(2,1)}), bf16[8,72,1024]{2,1,0:T(8,128)(2,1)S(1)}, u32[]{:S(2)}, u32[]{:S(2)}) async-start(bf16[8,72,1024]{2,1,0:T(8,128)(2,1)} %bitcast.148), calls=%async_computation.1 | async-start | bytes 2359296 | tf_op jit(solution)/shard_map/all_to_all | solution.py:93
  56.4 10.8 %reduce-scatter.5.cloned.1.call-start = ((), (), s32[]{:S(2)}) async-start(), calls=%async_computation.7 | async-start | bytes 17825792 | tf_op jit(solution)/shard_map/reduce_scatter | solution.py:111
  67.1 11.5 %multiply_convert_fusion.1 = (bf16[576,4096]{1,0:T(8,128)(2,1)}, f32[576,4096]{1,0:T(8,128)}) fusion(bf16[576,1024]{1,0:T(8,128)(2,1)} %bitcast.41, bf16[1,1024,4096]{2,1,0:T(8,128)(2,1)} %param.15), kind=kOutput, calls=%fused_computation.5 | convolution fusion | flops 4843634688 | bytes 23724032 | tf_op jit(solution)/shard_map/dot_general | solution.py:105
  78.7 12.6 %fusion.44 = f32[4096,1024]{1,0:T(8,128)} fusion(bf16[576,4096]{1,0:T(8,128)(2,1)} %get-tuple-element.17, bf16[576,1024]{1,0:T(8,128)(2,1)S(1)} %bitcast.151), kind=kOutput, calls=%fused_computation.179 | convolution fusion | flops 4831838208 | bytes 22675456 | tf_op jit(solution)/shard_map/dot_general | solution.py:33
  91.4 10.8 %multiply_convert_fusion = bf16[576,4096]{1,0:T(8,128)(2,1)S(1)} fusion(f32[576,4096]{1,0:T(8,128)} %get-tuple-element.16, bf16[576,1024]{1,0:T(8,128)(2,1)S(1)} %bitcast.152, bf16[1,4096,1024]{2,1,0:T(8,128)(2,1)} %param.16), kind=kOutput, calls=%fused_computation.4 | convolution fusion | flops 4853071872 | bytes 23724032 | tf_op jit(solution)/shard_map/dot_general | solution.py:39
  102.2 2.1 copy-done.8
  104.3 11.5 %fusion.45 = f32[1024,4096]{1,0:T(8,128)} fusion(bf16[576,1024]{1,0:T(8,128)(2,1)} %bitcast.41, bf16[576,4096]{1,0:T(8,128)(2,1)S(1)} %multiply_convert_fusion), kind=kOutput, calls=%fused_computation.180 | convolution fusion | flops 4831838208 | bytes 22675456 | tf_op jit(solution)/shard_map/dot_general | solution.py:33
  115.8 10.0 %fusion.24 = bf16[576,1024]{1,0:T(8,128)(2,1)} fusion(bf16[576,4096]{1,0:T(8,128)(2,1)} %get-tuple-element.17, bf16[1,4096,1024]{2,1,0:T(8,128)(2,1)} %param.16), kind=kOutput, calls=%fused_computation.110 | convolution fusion | flops 4832428032 | bytes 14286848 | tf_op jit(solution)/shard_map/dot_general | solution.py:112
  125.8 9.9 %fusion.21 = bf16[576,1024]{1,0:T(8,128)(2,1)} fusion(bf16[576,4096]{1,0:T(8,128)(2,1)} %copy-done.8, bf16[1,1024,4096]{2,1,0:T(8,128)(2,1)} %param.15), kind=kOutput, calls=%fused_computation.109 | convolution fusion | flops 4832428032 | bytes 14286848 | tf_op jit(solution)/shard_map/dot_general | solution.py:39
  135.7 5.1 %all-to-all-start.3 = ((bf16[8,72,1024]{2,1,0:T(8,128)(2,1)}), bf16[8,72,1024]{2,1,0:T(8,128)(2,1)S(1)}, u32[]{:S(2)}, u32[]{:S(2)}) async-start(bf16[8,72,1024]{2,1,0:T(8,128)(2,1)} %bitcast.153), calls=%async_computation.3 | async-start | bytes 2359296 | tf_op jit(solution)/shard_map/all_to_all | solution.py:127
  140.9 16.3 %all-to-all-done.3 = bf16[8,72,1024]{2,1,0:T(8,128)(2,1)S(1)} async-done(((bf16[8,72,1024]{2,1,0:T(8,128)(2,1)}), bf16[8,72,1024]{2,1,0:T(8,128)(2,1)S(1)}, u32[]{:S(2)}, u32[]{:S(2)}) %all-to-all-start.3) | async-done | bytes 1179680 | tf_op jit(solution)/shard_map/all_to_all | solution.py:127
  157.2 2.8 gather_fusion.1
  159.9 2.7 fusion.16
  162.7 2.0 add_add_fusion.1
  164.6 1.9 reduce_sum.384
  166.6 20.3 %multiply_reduce_fusion.30 = (f32[1024]{0:T(1024)S(1)}, f32[1024]{0:T(1024)S(1)}, f32[1024]{0:T(1024)S(1)}, f32[1024]{0:T(1024)S(1)}, f32[1024]{0:T(1024)S(1)}, ...) fusion(f32[2,256,1024]{2,1,0:T(8,128)} %copy-done.4, ...), kind=kLoop, calls=%fused_computation.98 | loop fusion | flops 27249664 | bytes 11610624 | tf_op jit(solution)/shard_map/transpose(jvp())/reduce_sum | solution.py:22
  186.9 4.9 %multiply_reduce_fusion.31 = (f32[1024]{0:T(1024)S(1)}, f32[1024]{0:T(1024)S(1)}, f32[1024]{0:T(1024)S(1)}, f32[1024]{0:T(1024)S(1)}, f32[1024]{0:T(1024)S(1)}, ...) fusion(f32[2,256,1024]{2,1,0:T(8,128)S(1)} %get-tuple-element.5, ...), kind=kLoop, calls=%fused_computation.99 | loop fusion | flops 18855936 | bytes 4268032 | tf_op jit(solution)/shard_map/transpose(jvp())/reduce_sum | solution.py:22
  192.1 9.2 %broadcast_multiply_fusion.1 = (f32[2,256,1024]{2,1,0:T(8,128)}, f32[2,256,1024]{2,1,0:T(8,128)}, f32[2,256,1024]{2,1,0:T(8,128)}, f32[2,256,1024]{2,1,0:T(8,128...) fusion(f32[2,256,1024]{2,1,0:T(8,128)S(1)} %get-tuple-element.5, ...), kind=kLoop, calls=%fused_computation.114 | loop fusion | flops 6815744 | bytes 29413376 | tf_op jit(solution)/shard_map/transpose(jvp())/mul | solution.py:22
  201.3 12.4 %broadcast_multiply_fusion = (f32[2,256,1024]{2,1,0:T(8,128)}, f32[2,256,1024]{2,1,0:T(8,128)}, f32[2,256,1024]{2,1,0:T(8,128)}, f32[2,256,1024]{2,1,0:T(8,128)}...) fusion(f32[2,256,1024]{2,1,0:T(8,128)S(1)} %get-tuple-element.5, ...), kind=kLoop, calls=%fused_computation.113 | loop fusion | flops 9437184 | bytes 39919616 | tf_op jit(solution)/shard_map/transpose(jvp())/mul | solution.py:22
  213.7 22.6 %pad_add_fusion = f32[2,286,1024]{2,1,0:T(8,128)} fusion(f32[2,256,1024]{2,1,0:T(8,128)} %get-tuple-element.72, f32[2,256,1024]{2,1,0:T(8,128)} %get-tuple-element.73, f32[2,256,1024]{2,1,0:T(8,128)} %get-tuple-element.74, f32[2,256,1024]{2,1,0:T(8,128)} %get-tuple-element.75, f32[2,256,1024]{2,1,0:T(8,128)} %get-tuple-element.76, ...), kind=kLoop, calls=%fused_computation.17 | loop fusion | flops 14057472 | bytes 54771712 | tf_op jit(solution)/shard_map/transpose(jvp())/add_any | solution.py:22
  236.3 6.8 %multiply_reduce_fusion.32 = (f32[2,256]{1,0:T(2,128)S(1)}, f32[2,256,1024]{2,1,0:T(8,128)S(1)}, f32[2,256,1024]{2,1,0:T(8,128)S(1)}) fusion(f32[1024]{0:T(1024)S(1)} %copy-done.10, f32[2,256]{1,0:T(2,128)S(1)} %div.56, bf16[2,256,1024]{2,1,0:T(8,128)(2,1)S(1)} %bitcast.146, f32[2,256]{1,0:T(2,128)S(1)} %get-tuple-element.129, ...), kind=kLoop, calls=%fused_computation.101 | loop fusion | flops 6290944 | bytes 19933184 | tf_op jit(solution)/shard_map/transpose(jvp())/reduce_sum | solution.py:11
  243.2 1.1 multiply_reduce_fusion
  244.5 1.4 collective-permute-start
  245.9 8.1 %collective-permute-done = f32[33,1024]{1,0:T(8,128)S(1)} collective-permute-done((f32[33,1024]{1,0:T(8,128)S(1)}, f32[33,1024]{1,0:T(8,128)S(1)}, u32[]{:S(2)}, u32[]{:S(2)}) %collective-permute-start) | collective-permute-done | bytes 135200 | tf_op jit(solution)/shard_map/ppermute | solution.py:50
  254.1 3.1 collective-permute-start.1
  257.2 7.8 %collective-permute-done.1 = f32[33,1024]{1,0:T(8,128)S(1)} collective-permute-done((f32[33,1024]{1,0:T(8,128)S(1)}, f32[33,1024]{1,0:T(8,128)S(1)}, u32[]{:S(2)}, u32[]{:S(2)}) %collective-permute-start.1) | collective-permute-done | bytes 135200 | tf_op jit(solution)/shard_map/ppermute | solution.py:50
  265.0 1.3 collective-permute-start.2
  266.2 6.0 %all-to-all-start.2 = ((bf16[8,72,1024]{2,1,0:T(8,128)(2,1)}), bf16[8,72,1024]{2,1,0:T(8,128)(2,1)S(1)}, u32[]{:S(2)}, u32[]{:S(2)}) async-start(bf16[8,72,1024]{2,1,0:T(8,128)(2,1)} %bitcast.150), calls=%async_computation.2 | async-start | bytes 2359296 | tf_op jit(solution)/shard_map/all_to_all | solution.py:120
  272.3 1.1 add.381
  273.3 2.6 collective-permute-start.3
  275.9 7.6 %collective-permute-done.3 = f32[33,1024]{1,0:T(8,128)S(1)} collective-permute-done((f32[33,1024]{1,0:T(8,128)S(1)}, f32[33,1024]{1,0:T(8,128)S(1)}, u32[]{:S(2)}, u32[]{:S(2)}) %collective-permute-start.3) | collective-permute-done | bytes 135200 | tf_op jit(solution)/shard_map/ppermute | solution.py:50
  283.5 4.6 %collective-permute-start.4 = (f32[33,1024]{1,0:T(8,128)S(1)}, f32[33,1024]{1,0:T(8,128)S(1)}, u32[]{:S(2)}, u32[]{:S(2)}) collective-permute-start(f32[33,1024]{1,0:T(8,128)S(1)} %add.382), channel_id=1, source_target_pairs={{0,1},{1,0},{2,3},{3,2},{4,5},{5,4},{6,7},{7,6},{8,9},{9,8},{10,11... | collective-permute-start | bytes 405512 | tf_op jit(solution)/shard_map/ppermute | solution.py:50
  289.2 1.0 collective-permute-start.5
  290.2 4.0 %add_convert_fusion = bf16[2,256,1024]{2,1,0:T(8,128)(2,1)} fusion(f32[2,256]{1,0:T(2,128)S(1)} %negate_multiply_fusion, f32[2,256]{1,0:T(2,128)S(1)} %negate_multiply_fusion.1, f32[2,256]{1,0:T(2,128)S(1)} %multiply_multiply_fusion.1, f32[2,256]{1,0:T(2,128)S(1)} %div.56, f32[2,256]{1,0:T(2,128)S(1)} %rsqrt.22, f32[2,256,1024]{2,1,0:T(8,128)} %copy-done.6, ...), kind=kLoop, calls=%fused_computation.100 | loop fusion | flops 11010048 | bytes 8413696 | tf_op jit(solution)/shard_map/convert_element_type | solution.py:165
  294.2 2.8 gather_fusion
  297.9 1.9 collective-permute-start.6
  299.7 2.8 fusion.18
  302.5 2.1 collective-permute-done.6
  305.9 23.2 %reduce-scatter.3.cloned.1.call-done = f32[1024,256]{1,0:T(8,128)} async-done(((f32[1024,4096]{1,0:T(8,128)}), f32[1024,256]{1,0:T(8,128)}) %reduce-scatter.3.cloned.1.call-update) | async-done | bytes 1048592 | tf_op jit(solution)/shard_map/reduce_scatter | solution.py:117
  (82 shorter events, 5.7 us)
Async XLA Ops:
  7.2 5.1 %copy-start = (bf16[512,1024]{1,0:T(8,128)(2,1)S(1)}, bf16[512,1024]{1,0:T(8,128)(2,1)}, u32[]{:S(2)}) copy-start(bf16[512,1024]{1,0:T(8,128)(2,1)} %param.9) | copy-start | bytes 3145732
  7.2 3.2 copy-start.9
  7.2 3.4 %copy-start.17 = (s32[2]{0:T(128)S(1)}, s32[2]{0:T(128)}, u32[]{:S(2)}) copy-start(s32[2]{0:T(128)} %param.10) | copy-start | bytes 28
  7.2 3.5 %copy-start.14 = (s32[512,1]{0,1:T(1,128)S(1)}, s32[512,1]{0,1:T(1,128)}, u32[]{:S(2)}) copy-start(s32[512,1]{0,1:T(1,128)} %param.11) | copy-start | bytes 6148
  7.2 5.0 %copy-start.10 = (f32[1024]{0:T(1024)S(1)}, f32[1024]{0:T(1024)}, u32[]{:S(2)}) copy-start(f32[1024]{0:T(1024)} %param.13) | copy-start | bytes 12292
  10.5 11.7 %copy-start.12 = (f32[2,256]{1,0:T(2,128)}, f32[2,256]{1,0:T(2,128)S(1)}, u32[]{:S(2)}) copy-start(f32[2,256]{1,0:T(2,128)S(1)} %add.338) | copy-start | bytes 6148
  12.7 9.6 %copy-start.4 = (f32[2,256,1024]{2,1,0:T(8,128)}, f32[2,256,1024]{2,1,0:T(8,128)S(1)}, u32[]{:S(2)}) copy-start(f32[2,256,1024]{2,1,0:T(8,128)S(1)} %multiply_multiply_fusion) | copy-start | bytes 6291460
  22.3 0.7 copy-start.11
  24.3 11.2 %copy-start.7 = (bf16[512,1024]{1,0:T(8,128)(2,1)S(1)}, bf16[512,1024]{1,0:T(8,128)(2,1)}, u32[]{:S(2)}) copy-start(bf16[512,1024]{1,0:T(8,128)(2,1)} %param.17) | copy-start | bytes 3145732
  28.6 23.3 %all-to-all-start = ((bf16[8,72,1024]{2,1,0:T(8,128)(2,1)}), bf16[8,72,1024]{2,1,0:T(8,128)(2,1)}, u32[]{:S(2)}, u32[]{:S(2)}) async-start(bf16[8,72,1024]{2,1,0:T(8,128)(2,1)} %bitcast.149), calls=%async_computation | async-start | bytes 2359296 | tf_op jit(solution)/shard_map/all_to_all | solution.py:86
  35.5 16.5 %copy-start.15 = (pred[512]{0:T(512)(128)(4,1)}, pred[512]{0:T(512)(128)(4,1)S(1)}, u32[]{:S(2)}) copy-start(pred[512]{0:T(512)(128)(4,1)S(1)} %gt.26) | copy-start | bytes 1540
  51.9 26.7 %all-to-all-start.1 = ((bf16[8,72,1024]{2,1,0:T(8,128)(2,1)}), bf16[8,72,1024]{2,1,0:T(8,128)(2,1)S(1)}, u32[]{:S(2)}, u32[]{:S(2)}) async-start(bf16[8,72,1024]{2,1,0:T(8,128)(2,1)} %bitcast.148), calls=%async_computation.1 | async-start | bytes 2359296 | tf_op jit(solution)/shard_map/all_to_all | solution.py:93
  56.4 249.5 %reduce-scatter.5.cloned.1.call-start = ((), (), s32[]{:S(2)}) async-start(), calls=%async_computation.7 | async-start | bytes 17825792 | tf_op jit(solution)/shard_map/reduce_scatter | solution.py:111
  91.3 237.8 %reduce-scatter.3.cloned.1.call-start = ((), (), s32[]{:S(2)}) async-start(), calls=%async_computation.6 | async-start | bytes 17825792 | tf_op jit(solution)/shard_map/reduce_scatter | solution.py:117
  102.2 2.1 copy-start.8
  135.7 21.4 %all-to-all-start.3 = ((bf16[8,72,1024]{2,1,0:T(8,128)(2,1)}), bf16[8,72,1024]{2,1,0:T(8,128)(2,1)S(1)}, u32[]{:S(2)}, u32[]{:S(2)}) async-start(bf16[8,72,1024]{2,1,0:T(8,128)(2,1)} %bitcast.153), calls=%async_computation.3 | async-start | bytes 2359296 | tf_op jit(solution)/shard_map/all_to_all | solution.py:127
  159.9 2.7 copy-start.3
  164.6 2.0 copy-start.1
  166.6 20.3 %copy-start.5 = (f32[2,256,1024]{2,1,0:T(8,128)S(1)}, f32[2,256,1024]{2,1,0:T(8,128)}, u32[]{:S(2)}) copy-start(f32[2,256,1024]{2,1,0:T(8,128)} %copy-done.4) | copy-start | bytes 6291460
  236.3 6.8 %copy-start.13 = (f32[2,256]{1,0:T(2,128)S(1)}, f32[2,256]{1,0:T(2,128)}, u32[]{:S(2)}) copy-start(f32[2,256]{1,0:T(2,128)} %copy-done.12) | copy-start | bytes 6148
  243.1 1.3 copy-start.6
  244.5 9.6 %collective-permute-start = (f32[33,1024]{1,0:T(8,128)S(1)}, f32[33,1024]{1,0:T(8,128)S(1)}, u32[]{:S(2)}, u32[]{:S(2)}) collective-permute-start(f32[33,1024]{1,0:T(8,128)S(1)} %pad_maximum_fusion), channel_id=1, source_target_pairs={{0,8},{8,0},{16,24},{24,16},{32,40},{40,32},{48,56},{56,48},{64,72... | collective-permute-start | bytes 405512 | tf_op jit(solution)/shard_map/ppermute | solution.py:50
  254.1 10.9 %collective-permute-start.1 = (f32[33,1024]{1,0:T(8,128)S(1)}, f32[33,1024]{1,0:T(8,128)S(1)}, u32[]{:S(2)}, u32[]{:S(2)}) collective-permute-start(f32[33,1024]{1,0:T(8,128)S(1)} %fusion.39), channel_id=1, source_target_pairs={{0,16},{8,24},{16,0},{24,8},{32,48},{40,56},{48,32},{56,40},{64,80... | collective-permute-start | bytes 405512 | tf_op jit(solution)/shard_map/ppermute | solution.py:50
  265.0 7.3 %collective-permute-start.2 = (f32[33,1024]{1,0:T(8,128)S(1)}, f32[33,1024]{1,0:T(8,128)}, u32[]{:S(2)}, u32[]{:S(2)}) collective-permute-start(f32[33,1024]{1,0:T(8,128)S(1)} %add.380), channel_id=1, source_target_pairs={{0,32},{8,40},{16,48},{24,56},{32,0},{40,8},{48,16},{56,24},{64,96... | collective-permute-start | bytes 405512 | tf_op jit(solution)/shard_map/ppermute | solution.py:50
  266.2 27.9 %all-to-all-start.2 = ((bf16[8,72,1024]{2,1,0:T(8,128)(2,1)}), bf16[8,72,1024]{2,1,0:T(8,128)(2,1)S(1)}, u32[]{:S(2)}, u32[]{:S(2)}) async-start(bf16[8,72,1024]{2,1,0:T(8,128)(2,1)} %bitcast.150), calls=%async_computation.2 | async-start | bytes 2359296 | tf_op jit(solution)/shard_map/all_to_all | solution.py:120
  272.3 17.9 %copy-start.2 = (bf16[512,1024]{1,0:T(8,128)(2,1)S(1)}, bf16[512,1024]{1,0:T(8,128)(2,1)}, u32[]{:S(2)}) copy-start(bf16[512,1024]{1,0:T(8,128)(2,1)} %param.9) | copy-start | bytes 3145732
  273.3 10.2 %collective-permute-start.3 = (f32[33,1024]{1,0:T(8,128)S(1)}, f32[33,1024]{1,0:T(8,128)S(1)}, u32[]{:S(2)}, u32[]{:S(2)}) collective-permute-start(f32[33,1024]{1,0:T(8,128)S(1)} %add.381), channel_id=1, source_target_pairs={{0,64},{8,72},{16,80},{24,88},{32,96},{40,104},{48,112},{56,120},{... | collective-permute-start | bytes 405512 | tf_op jit(solution)/shard_map/ppermute | solution.py:50
  283.5 5.6 %collective-permute-start.4 = (f32[33,1024]{1,0:T(8,128)S(1)}, f32[33,1024]{1,0:T(8,128)S(1)}, u32[]{:S(2)}, u32[]{:S(2)}) collective-permute-start(f32[33,1024]{1,0:T(8,128)S(1)} %add.382), channel_id=1, source_target_pairs={{0,1},{1,0},{2,3},{3,2},{4,5},{5,4},{6,7},{7,6},{8,9},{9,8},{10,11... | collective-permute-start | bytes 405512 | tf_op jit(solution)/shard_map/ppermute | solution.py:50
  289.2 7.8 %collective-permute-start.5 = (f32[33,1024]{1,0:T(8,128)S(1)}, f32[33,1024]{1,0:T(8,128)}, u32[]{:S(2)}, u32[]{:S(2)}) collective-permute-start(f32[33,1024]{1,0:T(8,128)S(1)} %add.383), channel_id=1, source_target_pairs={{0,2},{1,3},{2,0},{3,1},{4,6},{5,7},{6,4},{7,5},{8,10},{9,11},{10,... | collective-permute-start | bytes 405512 | tf_op jit(solution)/shard_map/ppermute | solution.py:50
  294.2 5.6 %copy-start.16 = (pred[512]{0:T(512)(128)(4,1)S(1)}, pred[512]{0:T(512)(128)(4,1)}, u32[]{:S(2)}) copy-start(pred[512]{0:T(512)(128)(4,1)} %copy-done.15) | copy-start | bytes 1540
  297.9 6.7 %collective-permute-start.6 = (f32[33,1024]{1,0:T(8,128)S(1)}, f32[33,1024]{1,0:T(8,128)S(1)}, u32[]{:S(2)}, u32[]{:S(2)}) collective-permute-start(f32[33,1024]{1,0:T(8,128)S(1)} %add.384), channel_id=1, source_target_pairs={{0,4},{1,5},{2,6},{3,7},{4,0},{5,1},{6,2},{7,3},{8,12},{9,13},{10,... | collective-permute-start | bytes 405512 | tf_op jit(solution)/shard_map/ppermute | solution.py:50
Sparse Core Ops, SparseCore 0:
  91.4 111.2 reduce-scatter.4
  206.7 122.3 reduce-scatter.2

commit v2 on v1

--- a/solution.py
+++ b/solution.py
@@ -63,9 +63,6 @@
     live_mask = (jnp.arange(utt_len, dtype=jnp.int32)[None, :] < lengths[:, None]).astype(
         jnp.float32
     )[:, :, None]
-    frames_f = frames.astype(jnp.float32).reshape(utt_count, utt_len, feat_width)
-    residual, normed = conv_module(frames_f, live_mask, conv_kernel, conv_gain, ffn_gain)
-    expert_in = normed.reshape(frame_count, feat_width).astype(jnp.bfloat16)
     live_flat = live_mask.reshape(frame_count) > 0.5
     target = jnp.where(live_flat, expert_ids[:, 0], expert_count)
     one_hot = (target[:, None] == jnp.arange(expert_count, dtype=jnp.int32)[None, :]).astype(
@@ -74,29 +71,31 @@
     rank_in = jnp.sum((jnp.cumsum(one_hot, axis=0, dtype=jnp.int32) - 1) * one_hot, axis=1)
     dest_slot = jnp.where(live_flat, target * capacity + rank_in, slot_total)
     routed_grad = jnp.where(live_flat[:, None], out_grad, jnp.zeros_like(out_grad))
-    send_in = (
-        jnp.zeros((slot_total, feat_width), jnp.bfloat16).at[dest_slot].set(expert_in, mode="drop")
-    )
     send_grad = (
         jnp.zeros((slot_total, feat_width), jnp.bfloat16)
         .at[dest_slot]
         .set(routed_grad, mode="drop")
     )
-    recv_in, recv_grad = (
-        lax.all_to_all(
-            send_in.reshape(expert_count, capacity, feat_width),
-            "expert",
-            split_axis=0,
-            concat_axis=0,
-            tiled=True,
-        ),
-        lax.all_to_all(
-            send_grad.reshape(expert_count, capacity, feat_width),
-            "expert",
-            split_axis=0,
-            concat_axis=0,
-            tiled=True,
-        ),
+    recv_grad = lax.all_to_all(
+        send_grad.reshape(expert_count, capacity, feat_width),
+        "expert",
+        split_axis=0,
+        concat_axis=0,
+        tiled=True,
+    )
+    frames_f = frames.astype(jnp.float32).reshape(utt_count, utt_len, feat_width)
+    residual, normed = conv_module(frames_f, live_mask, conv_kernel, conv_gain, ffn_gain)
+    expert_in = normed.reshape(frame_count, feat_width).astype(jnp.bfloat16)
+    send_in = (
+        jnp.zeros((slot_total, feat_width), jnp.bfloat16).at[dest_slot].set(expert_in, mode="drop")
+    )
+    recv_grad, send_in = lax.optimization_barrier((recv_grad, send_in))
+    recv_in = lax.all_to_all(
+        send_in.reshape(expert_count, capacity, feat_width),
+        "expert",
+        split_axis=0,
+        concat_axis=0,
+        tiled=True,
     )
     routed_in = recv_in.reshape(slot_total, feat_width)
     grad_rows = recv_grad.reshape(slot_total, feat_width)

time: 340 us -> 341 us (level)
  blocking collectives: 0 us -> 31.8 us
  starting transfers between devices: 49.1 us -> 33.2 us
  waiting for transfers between devices: 78.9 us -> 68.1 us
    all_to_all x0 -> x1, blocking collectives: none -> 31.8 us  [shards(): lax.all_to_all(send_in.reshape(expert_count, capacity, feat_width), 'expe...]
    all_to_all x1 -> x0, waiting for transfers between devices: 12.7 us -> none  [shards(): lax.all_to_all(send_in.reshape(expert_count, capacity, feat_width), 'expe...]
    reduce_scatter x1, starting transfers between devices: 10.8 us -> 0.01 us  [shards(): grad_out = lax.psum_scatter(full_out, 'dp', scatter_dimension=0, tiled=True)]
    all_to_all x1 -> x0, starting transfers between devices: 6.8 us -> none  [shards(): lax.all_to_all(send_in.reshape(expert_count, capacity, feat_width), 'expe...]
  transfers between devices with their start and end apart: 13 -> 12, of which waited for: 8 -> 9; matrix products, arithmetic and copies ran while one was open for 47% -> 46% of each run, Pallas kernels for 0% -> 0%
where the time goes in v2:
time: 341 us; the launch traced here: 339 us
  other arithmetic  113 us (33%)
  waiting for transfers between devices  68.1 us (20%)
  matrix products  63.1 us (19%)
  starting transfers between devices  33.2 us (10%)
  blocking collectives  31.8 us (9%)
  local copies, waits for them, and re-layouts  15.5 us (5%)
  between operations  14.5 us (4%)
    all_to_all x1, blocking collectives, shards(): lax.all_to_all(send_in.reshape(expert_count, capacity, feat_width), 'expe...  31.8 us
    ppermute x7, waiting for transfers between devices, butterfly_sum(): values = values + lax.ppermute(values, axis_name, pairs)  26.7 us
    reduce_sum x2, other arithmetic, conv_module(): conv_kernel[tap_index] * padded[:, tap_index:tap_index + utt_len]  25.2 us
    reduce_scatter x1, waiting for transfers between devices, shards(): grad_in = lax.psum_scatter(full_in, 'dp', scatter_dimension=1, tiled=True)  24 us
    add_any x1, other arithmetic, conv_module(): padded[:, tap_index:tap_index + utt_len]  22.6 us
    dot_general x2, matrix products, contract_rows(): lax.dot_general(left_rows, right_rows, (((0,), (0,)), ((), ())), preferre...  21.7 us
    mul x2, other arithmetic, conv_module(): conv_kernel[tap_index] * padded[:, tap_index:tap_index + utt_len]  21.6 us
    dot_general x2, matrix products, times_transpose(): lax.dot_general(left_rows, matrix, (((1,), (1,)), ((), ())), preferred_el...  20.4 us
  transfers between devices with their start and end apart: 12, of which 9 were waited for; matrix products, arithmetic and copies ran while one was open for 46% of the time, Pallas kernels for 0%

profile of v2, /device:TPU:1, one launch (start us, length us, event | category | flops | bytes accessed | tf_op | source)
XLA Modules:
  0.0 338.7 jit_solution(2444811201278537264)
XLA Ops:
  7.2 0.7 broadcast_compare_fusion
  8.6 1.1 reduce-window.6
  10.1 0.7 compare_select_fusion
  10.8 4.5 %scatter_custom_fusion = bf16[576,1024]{1,0:T(8,128)(2,1)} fusion(s32[512]{0:T(512)S(1)} %bitcast.258, bf16[512,1024]{1,0:T(8,128)(2,1)} %param.17, pred[512]{0:T(512)(128)(4,1)S(1)} %gt.26, bf16[]{:T(256)} %constant.44.clone.1), kind=kCustom, calls=%fused_computation.111 | custom fusion | flops 524288 | bytes 2229760 | tf_op jit(solution)/shard_map/scatter | solution.py:77
  15.3 6.9 %all-to-all-start = ((bf16[8,72,1024]{2,1,0:T(8,128)(2,1)}), bf16[8,72,1024]{2,1,0:T(8,128)(2,1)}, u32[]{:S(2)}, u32[]{:S(2)}) async-start(bf16[8,72,1024]{2,1,0:T(8,128)(2,1)} %bitcast.39), calls=%async_computation | async-start | bytes 2359296 | tf_op jit(solution)/shard_map/all_to_all | solution.py:79
  23.6 9.6 %multiply_add_fusion = (f32[2,256,1024]{2,1,0:T(8,128)S(1)}, f32[2,256,1024]{2,1,0:T(8,128)}) fusion(f32[2,256]{1,0:T(2,128)S(1)} %get-tuple-element.133, bf16[512,1024]{1,0:T(8,128)(2,1)S(1)} %copy-done, f32[1024]{0:T(1024)S(1)} %bitcast.205, f32[1024]{0:T(1024)S(1)} %bitcast.159, f32[1024]{0:T(1024)S(1)} %bitcast.161, f32[1024]{0:T(1024)S(1)} %bitcast.163, ...), kind=kLoop, calls=%fused_computation.104 | loop fusion | flops 35651584 | bytes 7469056 | tf_op jit(solution)/shard_map/add | solution.py:23
  34.1 3.6 %scatter_custom_fusion.1 = bf16[576,1024]{1,0:T(8,128)(2,1)} fusion(s32[512]{0:T(512)S(1)} %bitcast.259, bf16[512,1024]{1,0:T(8,128)(2,1)S(1)} %bitcast.154, bf16[]{:T(256)} %constant.44.clone.1), kind=kCustom, calls=%fused_computation.146 | custom fusion | bytes 1179650 | tf_op jit(solution)/shard_map/scatter | solution.py:90
  37.7 1.0 all-to-all-done
  38.7 31.8 %all_to_all.20 = bf16[8,72,1024]{2,1,0:T(8,128)(2,1)S(1)} all-to-all(bf16[8,72,1024]{2,1,0:T(8,128)(2,1)} %bitcast.150), channel_id=1, replica_groups=mesh['dp'=16,'expert'=8] {'expert'}, dimensions={0} | all-to-all | bytes 2359296 | tf_op jit(solution)/shard_map/all_to_all | solution.py:93
  70.5 11.1 %multiply_convert_fusion.1 = (bf16[576,4096]{1,0:T(8,128)(2,1)S(1)}, f32[576,4096]{1,0:T(8,128)}) fusion(bf16[576,1024]{1,0:T(8,128)(2,1)S(1)} %bitcast.148, bf16[1,1024,4096]{2,1,0:T(8,128)(2,1)} %param.15), kind=kOutput, calls=%fused_computation.5 | convolution fusion | flops 4843634688 | bytes 23724032 | tf_op jit(solution)/shard_map/dot_general | solution.py:104
  81.6 2.2 copy-done.15
  83.8 11.5 %fusion.44 = f32[4096,1024]{1,0:T(8,128)} fusion(bf16[576,4096]{1,0:T(8,128)(2,1)S(1)} %get-tuple-element.21, bf16[576,1024]{1,0:T(8,128)(2,1)} %bitcast.44), kind=kOutput, calls=%fused_computation.179 | convolution fusion | flops 4831838208 | bytes 22675456 | tf_op jit(solution)/shard_map/dot_general | solution.py:33
  95.4 10.5 %multiply_convert_fusion = bf16[576,4096]{1,0:T(8,128)(2,1)S(1)} fusion(f32[576,4096]{1,0:T(8,128)} %get-tuple-element.20, bf16[576,1024]{1,0:T(8,128)(2,1)} %bitcast.44, bf16[1,4096,1024]{2,1,0:T(8,128)(2,1)} %param.16), kind=kOutput, calls=%fused_computation.4 | convolution fusion | flops 4853071872 | bytes 23724032 | tf_op jit(solution)/shard_map/dot_general | solution.py:39
  105.9 2.1 copy-done.7
  108.1 10.2 %fusion.45 = f32[1024,4096]{1,0:T(8,128)} fusion(bf16[576,1024]{1,0:T(8,128)(2,1)S(1)} %bitcast.149, bf16[576,4096]{1,0:T(8,128)(2,1)S(1)} %multiply_convert_fusion), kind=kOutput, calls=%fused_computation.180 | convolution fusion | flops 4831838208 | bytes 22675456 | tf_op jit(solution)/shard_map/dot_general | solution.py:33
  118.3 9.9 %fusion.24 = bf16[576,1024]{1,0:T(8,128)(2,1)} fusion(bf16[576,4096]{1,0:T(8,128)(2,1)} %copy-done.15, bf16[1,4096,1024]{2,1,0:T(8,128)(2,1)} %param.16), kind=kOutput, calls=%fused_computation.110 | convolution fusion | flops 4832428032 | bytes 14286848 | tf_op jit(solution)/shard_map/dot_general | solution.py:111
  128.2 9.9 %fusion.21 = bf16[576,1024]{1,0:T(8,128)(2,1)} fusion(bf16[576,4096]{1,0:T(8,128)(2,1)} %copy-done.7, bf16[1,1024,4096]{2,1,0:T(8,128)(2,1)} %param.15), kind=kOutput, calls=%fused_computation.109 | convolution fusion | flops 4832428032 | bytes 14286848 | tf_op jit(solution)/shard_map/dot_general | solution.py:39
  138.1 4.7 %all-to-all-start.3 = ((bf16[8,72,1024]{2,1,0:T(8,128)(2,1)}), bf16[8,72,1024]{2,1,0:T(8,128)(2,1)S(1)}, u32[]{:S(2)}, u32[]{:S(2)}) async-start(bf16[8,72,1024]{2,1,0:T(8,128)(2,1)} %bitcast.152), calls=%async_computation.3 | async-start | bytes 2359296 | tf_op jit(solution)/shard_map/all_to_all | solution.py:126
  142.8 16.3 %all-to-all-done.3 = bf16[8,72,1024]{2,1,0:T(8,128)(2,1)S(1)} async-done(((bf16[8,72,1024]{2,1,0:T(8,128)(2,1)}), bf16[8,72,1024]{2,1,0:T(8,128)(2,1)S(1)}, u32[]{:S(2)}, u32[]{:S(2)}) %all-to-all-start.3) | async-done | bytes 1179680 | tf_op jit(solution)/shard_map/all_to_all | solution.py:126
  159.2 2.8 gather_fusion.1
  161.9 2.7 fusion.16
  164.7 2.0 add_add_fusion.1
  166.6 1.9 reduce_sum.384
  168.6 20.3 %multiply_reduce_fusion.30 = (f32[1024]{0:T(1024)S(1)}, f32[1024]{0:T(1024)S(1)}, f32[1024]{0:T(1024)S(1)}, f32[1024]{0:T(1024)S(1)}, f32[1024]{0:T(1024)S(1)}, ...) fusion(f32[2,256,1024]{2,1,0:T(8,128)} %copy-done.4, ...), kind=kLoop, calls=%fused_computation.98 | loop fusion | flops 27249664 | bytes 11610624 | tf_op jit(solution)/shard_map/transpose(jvp())/reduce_sum | solution.py:22
  188.9 4.9 %multiply_reduce_fusion.31 = (f32[1024]{0:T(1024)S(1)}, f32[1024]{0:T(1024)S(1)}, f32[1024]{0:T(1024)S(1)}, f32[1024]{0:T(1024)S(1)}, f32[1024]{0:T(1024)S(1)}, ...) fusion(f32[2,256,1024]{2,1,0:T(8,128)S(1)} %get-tuple-element.6, ...), kind=kLoop, calls=%fused_computation.99 | loop fusion | flops 18855936 | bytes 4268032 | tf_op jit(solution)/shard_map/transpose(jvp())/reduce_sum | solution.py:22
  194.1 9.2 %broadcast_multiply_fusion.1 = (f32[2,256,1024]{2,1,0:T(8,128)}, f32[2,256,1024]{2,1,0:T(8,128)}, f32[2,256,1024]{2,1,0:T(8,128)}, f32[2,256,1024]{2,1,0:T(8,128...) fusion(f32[2,256,1024]{2,1,0:T(8,128)S(1)} %get-tuple-element.6, ...), kind=kLoop, calls=%fused_computation.114 | loop fusion | flops 6815744 | bytes 29413376 | tf_op jit(solution)/shard_map/transpose(jvp())/mul | solution.py:22
  203.3 12.4 %broadcast_multiply_fusion = (f32[2,256,1024]{2,1,0:T(8,128)}, f32[2,256,1024]{2,1,0:T(8,128)}, f32[2,256,1024]{2,1,0:T(8,128)}, f32[2,256,1024]{2,1,0:T(8,128)}...) fusion(f32[2,256,1024]{2,1,0:T(8,128)S(1)} %get-tuple-element.6, ...), kind=kLoop, calls=%fused_computation.113 | loop fusion | flops 9437184 | bytes 39919616 | tf_op jit(solution)/shard_map/transpose(jvp())/mul | solution.py:22
  215.7 22.6 %pad_add_fusion = f32[2,286,1024]{2,1,0:T(8,128)} fusion(f32[2,256,1024]{2,1,0:T(8,128)} %get-tuple-element.76, f32[2,256,1024]{2,1,0:T(8,128)} %get-tuple-element.77, f32[2,256,1024]{2,1,0:T(8,128)} %get-tuple-element.78, f32[2,256,1024]{2,1,0:T(8,128)} %get-tuple-element.79, f32[2,256,1024]{2,1,0:T(8,128)} %get-tuple-element.80, ...), kind=kLoop, calls=%fused_computation.17 | loop fusion | flops 14057472 | bytes 54771712 | tf_op jit(solution)/shard_map/transpose(jvp())/add_any | solution.py:22
  238.3 6.9 %multiply_reduce_fusion.32 = (f32[2,256]{1,0:T(2,128)S(1)}, f32[2,256,1024]{2,1,0:T(8,128)S(1)}, f32[2,256,1024]{2,1,0:T(8,128)S(1)}) fusion(f32[1024]{0:T(1024)S(1)} %copy-done.9, f32[2,256]{1,0:T(2,128)S(1)} %div.56, bf16[2,256,1024]{2,1,0:T(8,128)(2,1)S(1)} %bitcast.146, f32[2,256]{1,0:T(2,128)S(1)} %get-tuple-element.133, ...), kind=kLoop, calls=%fused_computation.101 | loop fusion | flops 6290944 | bytes 19933184 | tf_op jit(solution)/shard_map/transpose(jvp())/reduce_sum | solution.py:11
  245.2 1.1 multiply_reduce_fusion
  246.5 1.3 collective-permute-start
  247.8 8.3 %collective-permute-done = f32[33,1024]{1,0:T(8,128)S(1)} collective-permute-done((f32[33,1024]{1,0:T(8,128)S(1)}, f32[33,1024]{1,0:T(8,128)S(1)}, u32[]{:S(2)}, u32[]{:S(2)}) %collective-permute-start) | collective-permute-done | bytes 135200 | tf_op jit(solution)/shard_map/ppermute | solution.py:50
  256.1 3.0 collective-permute-start.1
  259.1 7.8 %collective-permute-done.1 = f32[33,1024]{1,0:T(8,128)S(1)} collective-permute-done((f32[33,1024]{1,0:T(8,128)S(1)}, f32[33,1024]{1,0:T(8,128)S(1)}, u32[]{:S(2)}, u32[]{:S(2)}) %collective-permute-start.1) | collective-permute-done | bytes 135200 | tf_op jit(solution)/shard_map/ppermute | solution.py:50
  266.9 1.3 collective-permute-start.2
  268.2 6.1 %all-to-all-start.2 = ((bf16[8,72,1024]{2,1,0:T(8,128)(2,1)}), bf16[8,72,1024]{2,1,0:T(8,128)(2,1)S(1)}, u32[]{:S(2)}, u32[]{:S(2)}) async-start(bf16[8,72,1024]{2,1,0:T(8,128)(2,1)} %bitcast.151), calls=%async_computation.2 | async-start | bytes 2359296 | tf_op jit(solution)/shard_map/all_to_all | solution.py:119
  274.5 1.2 add.381
  275.7 2.3 collective-permute-start.3
  278.0 7.8 %collective-permute-done.3 = f32[33,1024]{1,0:T(8,128)S(1)} collective-permute-done((f32[33,1024]{1,0:T(8,128)S(1)}, f32[33,1024]{1,0:T(8,128)S(1)}, u32[]{:S(2)}, u32[]{:S(2)}) %collective-permute-start.3) | collective-permute-done | bytes 135200 | tf_op jit(solution)/shard_map/ppermute | solution.py:50
  285.8 4.6 %collective-permute-start.4 = (f32[33,1024]{1,0:T(8,128)S(1)}, f32[33,1024]{1,0:T(8,128)S(1)}, u32[]{:S(2)}, u32[]{:S(2)}) collective-permute-start(f32[33,1024]{1,0:T(8,128)S(1)} %add.382), channel_id=1, source_target_pairs={{0,1},{1,0},{2,3},{3,2},{4,5},{5,4},{6,7},{7,6},{8,9},{9,8},{10,11... | collective-permute-start | bytes 405512 | tf_op jit(solution)/shard_map/ppermute | solution.py:50
  290.3 1.0 collective-permute-done.4
  292.1 3.9 %add_convert_fusion = bf16[2,256,1024]{2,1,0:T(8,128)(2,1)} fusion(f32[2,256]{1,0:T(2,128)S(1)} %negate_multiply_fusion, f32[2,256]{1,0:T(2,128)S(1)} %negate_multiply_fusion.1, f32[2,256]{1,0:T(2,128)S(1)} %multiply_multiply_fusion.1, f32[2,256]{1,0:T(2,128)S(1)} %div.56, f32[2,256]{1,0:T(2,128)S(1)} %rsqrt.22, f32[2,256,1024]{2,1,0:T(8,128)} %copy-done.6, ...), kind=kLoop, calls=%fused_computation.100 | loop fusion | flops 11010048 | bytes 8413696 | tf_op jit(solution)/shard_map/convert_element_type | solution.py:164
  296.0 2.8 gather_fusion
  298.8 0.9 add.384
  299.7 2.3 collective-permute-start.6
  302.0 2.8 fusion.18
  304.8 1.6 collective-permute-done.6
  307.7 24.0 %reduce-scatter.3.cloned.1.call-done = f32[1024,256]{1,0:T(8,128)} async-done(((f32[1024,4096]{1,0:T(8,128)}), f32[1024,256]{1,0:T(8,128)}) %reduce-scatter.3.cloned.1.call-update) | async-done | bytes 1048592 | tf_op jit(solution)/shard_map/reduce_scatter | solution.py:116
  (77 shorter events, 6.2 us)
Async XLA Ops:
  7.9 7.4 %copy-start.13 = (pred[512]{0:T(512)(128)(4,1)}, pred[512]{0:T(512)(128)(4,1)S(1)}, u32[]{:S(2)}) copy-start(pred[512]{0:T(512)(128)(4,1)S(1)} %gt.26) | copy-start | bytes 1540
  10.8 11.4 %copy-start = (bf16[512,1024]{1,0:T(8,128)(2,1)S(1)}, bf16[512,1024]{1,0:T(8,128)(2,1)}, u32[]{:S(2)}) copy-start(bf16[512,1024]{1,0:T(8,128)(2,1)} %param.9) | copy-start | bytes 3145732
  15.3 7.6 %copy-start.8 = (f32[31,1024]{1,0:T(8,128)S(1)}, f32[31,1024]{1,0:T(8,128)}, u32[]{:S(2)}) copy-start(f32[31,1024]{1,0:T(8,128)} %param.12) | copy-start | bytes 380932
  15.3 7.8 %copy-start.9 = (f32[1024]{0:T(1024)S(1)}, f32[1024]{0:T(1024)}, u32[]{:S(2)}) copy-start(f32[1024]{0:T(1024)} %param.13) | copy-start | bytes 12292
  15.3 23.4 %all-to-all-start = ((bf16[8,72,1024]{2,1,0:T(8,128)(2,1)}), bf16[8,72,1024]{2,1,0:T(8,128)(2,1)}, u32[]{:S(2)}, u32[]{:S(2)}) async-start(bf16[8,72,1024]{2,1,0:T(8,128)(2,1)} %bitcast.39), calls=%async_computation | async-start | bytes 2359296 | tf_op jit(solution)/shard_map/all_to_all | solution.py:79
  22.3 285.4 %reduce-scatter.5.cloned.1.call-start = ((), (), s32[]{:S(2)}) async-start(), calls=%async_computation.7 | async-start | bytes 17825792 | tf_op jit(solution)/shard_map/reduce_scatter | solution.py:110
  23.1 10.0 %copy-start.11 = (f32[2,256]{1,0:T(2,128)}, f32[2,256]{1,0:T(2,128)S(1)}, u32[]{:S(2)}) copy-start(f32[2,256]{1,0:T(2,128)S(1)} %add.338) | copy-start | bytes 6148
  23.5 9.6 %copy-start.4 = (f32[2,256,1024]{2,1,0:T(8,128)}, f32[2,256,1024]{2,1,0:T(8,128)S(1)}, u32[]{:S(2)}) copy-start(f32[2,256,1024]{2,1,0:T(8,128)S(1)} %multiply_multiply_fusion) | copy-start | bytes 6291460
  33.1 0.7 copy-start.10
  81.6 2.2 copy-start.15
  95.4 236.3 %reduce-scatter.3.cloned.1.call-start = ((), (), s32[]{:S(2)}) async-start(), calls=%async_computation.6 | async-start | bytes 17825792 | tf_op jit(solution)/shard_map/reduce_scatter | solution.py:116
  105.9 2.1 copy-start.7
  138.1 21.1 %all-to-all-start.3 = ((bf16[8,72,1024]{2,1,0:T(8,128)(2,1)}), bf16[8,72,1024]{2,1,0:T(8,128)(2,1)S(1)}, u32[]{:S(2)}, u32[]{:S(2)}) async-start(bf16[8,72,1024]{2,1,0:T(8,128)(2,1)} %bitcast.152), calls=%async_computation.3 | async-start | bytes 2359296 | tf_op jit(solution)/shard_map/all_to_all | solution.py:126
  161.9 2.7 copy-start.3
  166.6 2.0 copy-start.1
  168.6 20.3 %copy-start.5 = (f32[2,256,1024]{2,1,0:T(8,128)S(1)}, f32[2,256,1024]{2,1,0:T(8,128)}, u32[]{:S(2)}) copy-start(f32[2,256,1024]{2,1,0:T(8,128)} %copy-done.4) | copy-start | bytes 6291460
  238.3 6.9 %copy-start.12 = (f32[2,256]{1,0:T(2,128)S(1)}, f32[2,256]{1,0:T(2,128)}, u32[]{:S(2)}) copy-start(f32[2,256]{1,0:T(2,128)} %copy-done.11) | copy-start | bytes 6148
  245.1 1.3 copy-start.6
  246.5 9.6 %collective-permute-start = (f32[33,1024]{1,0:T(8,128)S(1)}, f32[33,1024]{1,0:T(8,128)S(1)}, u32[]{:S(2)}, u32[]{:S(2)}) collective-permute-start(f32[33,1024]{1,0:T(8,128)S(1)} %pad_maximum_fusion), channel_id=1, source_target_pairs={{0,8},{8,0},{16,24},{24,16},{32,40},{40,32},{48,56},{56,48},{64,72... | collective-permute-start | bytes 405512 | tf_op jit(solution)/shard_map/ppermute | solution.py:50
  256.1 10.8 %collective-permute-start.1 = (f32[33,1024]{1,0:T(8,128)S(1)}, f32[33,1024]{1,0:T(8,128)S(1)}, u32[]{:S(2)}, u32[]{:S(2)}) collective-permute-start(f32[33,1024]{1,0:T(8,128)S(1)} %fusion.39), channel_id=1, source_target_pairs={{0,16},{8,24},{16,0},{24,8},{32,48},{40,56},{48,32},{56,40},{64,80... | collective-permute-start | bytes 405512 | tf_op jit(solution)/shard_map/ppermute | solution.py:50
  266.9 7.6 %collective-permute-start.2 = (f32[33,1024]{1,0:T(8,128)S(1)}, f32[33,1024]{1,0:T(8,128)}, u32[]{:S(2)}, u32[]{:S(2)}) collective-permute-start(f32[33,1024]{1,0:T(8,128)S(1)} %add.380), channel_id=1, source_target_pairs={{0,32},{8,40},{16,48},{24,56},{32,0},{40,8},{48,16},{56,24},{64,96... | collective-permute-start | bytes 405512 | tf_op jit(solution)/shard_map/ppermute | solution.py:50
  268.2 27.8 %all-to-all-start.2 = ((bf16[8,72,1024]{2,1,0:T(8,128)(2,1)}), bf16[8,72,1024]{2,1,0:T(8,128)(2,1)S(1)}, u32[]{:S(2)}, u32[]{:S(2)}) async-start(bf16[8,72,1024]{2,1,0:T(8,128)(2,1)} %bitcast.151), calls=%async_computation.2 | async-start | bytes 2359296 | tf_op jit(solution)/shard_map/all_to_all | solution.py:119
  274.3 17.8 %copy-start.2 = (bf16[512,1024]{1,0:T(8,128)(2,1)S(1)}, bf16[512,1024]{1,0:T(8,128)(2,1)}, u32[]{:S(2)}) copy-start(bf16[512,1024]{1,0:T(8,128)(2,1)} %param.9) | copy-start | bytes 3145732
  275.7 10.0 %collective-permute-start.3 = (f32[33,1024]{1,0:T(8,128)S(1)}, f32[33,1024]{1,0:T(8,128)S(1)}, u32[]{:S(2)}, u32[]{:S(2)}) collective-permute-start(f32[33,1024]{1,0:T(8,128)S(1)} %add.381), channel_id=1, source_target_pairs={{0,64},{8,72},{16,80},{24,88},{32,96},{40,104},{48,112},{56,120},{... | collective-permute-start | bytes 405512 | tf_op jit(solution)/shard_map/ppermute | solution.py:50
  285.8 5.6 %collective-permute-start.4 = (f32[33,1024]{1,0:T(8,128)S(1)}, f32[33,1024]{1,0:T(8,128)S(1)}, u32[]{:S(2)}, u32[]{:S(2)}) collective-permute-start(f32[33,1024]{1,0:T(8,128)S(1)} %add.382), channel_id=1, source_target_pairs={{0,1},{1,0},{2,3},{3,2},{4,5},{5,4},{6,7},{7,6},{8,9},{9,8},{10,11... | collective-permute-start | bytes 405512 | tf_op jit(solution)/shard_map/ppermute | solution.py:50
  291.4 7.4 %collective-permute-start.5 = (f32[33,1024]{1,0:T(8,128)S(1)}, f32[33,1024]{1,0:T(8,128)}, u32[]{:S(2)}, u32[]{:S(2)}) collective-permute-start(f32[33,1024]{1,0:T(8,128)S(1)} %add.383), channel_id=1, source_target_pairs={{0,2},{1,3},{2,0},{3,1},{4,6},{5,7},{6,4},{7,5},{8,10},{9,11},{10,... | collective-permute-start | bytes 405512 | tf_op jit(solution)/shard_map/ppermute | solution.py:50
  296.0 6.0 %copy-start.14 = (pred[512]{0:T(512)(128)(4,1)S(1)}, pred[512]{0:T(512)(128)(4,1)}, u32[]{:S(2)}) copy-start(pred[512]{0:T(512)(128)(4,1)} %copy-done.13) | copy-start | bytes 1540
  299.7 6.7 %collective-permute-start.6 = (f32[33,1024]{1,0:T(8,128)S(1)}, f32[33,1024]{1,0:T(8,128)S(1)}, u32[]{:S(2)}, u32[]{:S(2)}) collective-permute-start(f32[33,1024]{1,0:T(8,128)S(1)} %add.384), channel_id=1, source_target_pairs={{0,4},{1,5},{2,6},{3,7},{4,0},{5,1},{6,2},{7,3},{8,12},{9,13},{10,... | collective-permute-start | bytes 405512 | tf_op jit(solution)/shard_map/ppermute | solution.py:50
Sparse Core Ops, SparseCore 0:
  95.5 109.9 reduce-scatter.4
  209.4 122.2 reduce-scatter.2

commit v3 on v2

--- a/solution.py
+++ b/solution.py
@@ -157,7 +157,7 @@
     )
     tap_count = kernel_part.shape[0]
     small_grads = butterfly_sum(
-        jnp.concatenate([kernel_part, conv_part[None], ffn_part[None]], axis=0), ("dp", "expert")
+        jnp.concatenate([kernel_part, conv_part[None], ffn_part[None]], axis=0), ("expert", "dp")
     )
     kernel_grad = small_grads[:tap_count]
     gain_grads = small_grads[tap_count:]

time: 341 us -> 340 us (level)
  starting transfers between devices: 33.2 us -> 28.1 us
  waiting for transfers between devices: 68.1 us -> 71.8 us
    reduce_scatter x1, waiting for transfers between devices: 24 us -> 29.3 us  [shards(): grad_in = lax.psum_scatter(full_in, 'dp', scatter_dimension=1, tiled=True)]
    ppermute x7, starting transfers between devices: 15.4 us -> 11.5 us  [butterfly_sum(): values = values + lax.ppermute(values, axis_name, pairs)]
where the time goes in v3:
time: 340 us; the launch traced here: 337 us
  other arithmetic  112 us (33%)
  waiting for transfers between devices  71.8 us (21%)
  matrix products  63.1 us (19%)
  blocking collectives  31.8 us (9%)
  starting transfers between devices  28.1 us (8%)
  local copies, waits for them, and re-layouts  15.5 us (5%)
  between operations  14.5 us (4%)
    all_to_all x1, blocking collectives, shards(): lax.all_to_all(send_in.reshape(expert_count, capacity, feat_width), 'expe...  31.8 us
    reduce_scatter x1, waiting for transfers between devices, shards(): grad_in = lax.psum_scatter(full_in, 'dp', scatter_dimension=1, tiled=True)  29.3 us
    reduce_sum x2, other arithmetic, conv_module(): conv_kernel[tap_index] * padded[:, tap_index:tap_index + utt_len]  25.2 us
    ppermute x7, waiting for transfers between devices, butterfly_sum(): values = values + lax.ppermute(values, axis_name, pairs)  25.1 us
    add_any x1, other arithmetic, conv_module(): padded[:, tap_index:tap_index + utt_len]  22.6 us
    dot_general x2, matrix products, contract_rows(): lax.dot_general(left_rows, right_rows, (((0,), (0,)), ((), ())), preferre...  21.7 us
    mul x2, other arithmetic, conv_module(): conv_kernel[tap_index] * padded[:, tap_index:tap_index + utt_len]  21.6 us
    dot_general x2, matrix products, times_transpose(): lax.dot_general(left_rows, matrix, (((1,), (1,)), ((), ())), preferred_el...  20.4 us
  transfers between devices with their start and end apart: 12, of which 9 were waited for; matrix products, arithmetic and copies ran while one was open for 46% of the time, Pallas kernels for 0%

profile of v3, /device:TPU:1, one launch (start us, length us, event | category | flops | bytes accessed | tf_op | source)
XLA Modules:
  0.0 337.2 jit_solution(6464658382456067869)
XLA Ops:
  7.2 0.7 broadcast_compare_fusion
  8.6 1.1 reduce-window.6
  10.1 0.7 compare_select_fusion
  10.8 4.5 %scatter_custom_fusion = bf16[576,1024]{1,0:T(8,128)(2,1)} fusion(s32[512]{0:T(512)S(1)} %bitcast.258, bf16[512,1024]{1,0:T(8,128)(2,1)} %param.17, pred[512]{0:T(512)(128)(4,1)S(1)} %gt.26, bf16[]{:T(256)} %constant.44.clone.1), kind=kCustom, calls=%fused_computation.111 | custom fusion | flops 524288 | bytes 2229760 | tf_op jit(solution)/shard_map/scatter | solution.py:77
  15.3 6.9 %all-to-all-start = ((bf16[8,72,1024]{2,1,0:T(8,128)(2,1)}), bf16[8,72,1024]{2,1,0:T(8,128)(2,1)}, u32[]{:S(2)}, u32[]{:S(2)}) async-start(bf16[8,72,1024]{2,1,0:T(8,128)(2,1)} %bitcast.39), calls=%async_computation | async-start | bytes 2359296 | tf_op jit(solution)/shard_map/all_to_all | solution.py:79
  23.6 9.6 %multiply_add_fusion = (f32[2,256,1024]{2,1,0:T(8,128)S(1)}, f32[2,256,1024]{2,1,0:T(8,128)}) fusion(f32[2,256]{1,0:T(2,128)S(1)} %get-tuple-element.133, bf16[512,1024]{1,0:T(8,128)(2,1)S(1)} %copy-done, f32[1024]{0:T(1024)S(1)} %bitcast.205, f32[1024]{0:T(1024)S(1)} %bitcast.159, f32[1024]{0:T(1024)S(1)} %bitcast.161, f32[1024]{0:T(1024)S(1)} %bitcast.163, ...), kind=kLoop, calls=%fused_computation.104 | loop fusion | flops 35651584 | bytes 7469056 | tf_op jit(solution)/shard_map/add | solution.py:23
  34.1 3.6 %scatter_custom_fusion.1 = bf16[576,1024]{1,0:T(8,128)(2,1)} fusion(s32[512]{0:T(512)S(1)} %bitcast.259, bf16[512,1024]{1,0:T(8,128)(2,1)S(1)} %bitcast.154, bf16[]{:T(256)} %constant.44.clone.1), kind=kCustom, calls=%fused_computation.146 | custom fusion | bytes 1179650 | tf_op jit(solution)/shard_map/scatter | solution.py:90
  37.7 1.0 all-to-all-done
  38.7 31.8 %all_to_all.20 = bf16[8,72,1024]{2,1,0:T(8,128)(2,1)S(1)} all-to-all(bf16[8,72,1024]{2,1,0:T(8,128)(2,1)} %bitcast.150), channel_id=1, replica_groups=mesh['dp'=16,'expert'=8] {'expert'}, dimensions={0} | all-to-all | bytes 2359296 | tf_op jit(solution)/shard_map/all_to_all | solution.py:93
  70.5 11.1 %multiply_convert_fusion.1 = (bf16[576,4096]{1,0:T(8,128)(2,1)S(1)}, f32[576,4096]{1,0:T(8,128)}) fusion(bf16[576,1024]{1,0:T(8,128)(2,1)S(1)} %bitcast.148, bf16[1,1024,4096]{2,1,0:T(8,128)(2,1)} %param.15), kind=kOutput, calls=%fused_computation.5 | convolution fusion | flops 4843634688 | bytes 23724032 | tf_op jit(solution)/shard_map/dot_general | solution.py:104
  81.6 2.2 copy-done.15
  83.8 11.5 %fusion.44 = f32[4096,1024]{1,0:T(8,128)} fusion(bf16[576,4096]{1,0:T(8,128)(2,1)S(1)} %get-tuple-element.21, bf16[576,1024]{1,0:T(8,128)(2,1)} %bitcast.44), kind=kOutput, calls=%fused_computation.179 | convolution fusion | flops 4831838208 | bytes 22675456 | tf_op jit(solution)/shard_map/dot_general | solution.py:33
  95.4 10.5 %multiply_convert_fusion = bf16[576,4096]{1,0:T(8,128)(2,1)S(1)} fusion(f32[576,4096]{1,0:T(8,128)} %get-tuple-element.20, bf16[576,1024]{1,0:T(8,128)(2,1)} %bitcast.44, bf16[1,4096,1024]{2,1,0:T(8,128)(2,1)} %param.16), kind=kOutput, calls=%fused_computation.4 | convolution fusion | flops 4853071872 | bytes 23724032 | tf_op jit(solution)/shard_map/dot_general | solution.py:39
  105.9 2.1 copy-done.7
  108.1 10.2 %fusion.45 = f32[1024,4096]{1,0:T(8,128)} fusion(bf16[576,1024]{1,0:T(8,128)(2,1)S(1)} %bitcast.149, bf16[576,4096]{1,0:T(8,128)(2,1)S(1)} %multiply_convert_fusion), kind=kOutput, calls=%fused_computation.180 | convolution fusion | flops 4831838208 | bytes 22675456 | tf_op jit(solution)/shard_map/dot_general | solution.py:33
  118.3 9.9 %fusion.24 = bf16[576,1024]{1,0:T(8,128)(2,1)} fusion(bf16[576,4096]{1,0:T(8,128)(2,1)} %copy-done.15, bf16[1,4096,1024]{2,1,0:T(8,128)(2,1)} %param.16), kind=kOutput, calls=%fused_computation.110 | convolution fusion | flops 4832428032 | bytes 14286848 | tf_op jit(solution)/shard_map/dot_general | solution.py:111
  128.2 9.9 %fusion.21 = bf16[576,1024]{1,0:T(8,128)(2,1)} fusion(bf16[576,4096]{1,0:T(8,128)(2,1)} %copy-done.7, bf16[1,1024,4096]{2,1,0:T(8,128)(2,1)} %param.15), kind=kOutput, calls=%fused_computation.109 | convolution fusion | flops 4832428032 | bytes 14286848 | tf_op jit(solution)/shard_map/dot_general | solution.py:39
  138.1 4.7 %all-to-all-start.3 = ((bf16[8,72,1024]{2,1,0:T(8,128)(2,1)}), bf16[8,72,1024]{2,1,0:T(8,128)(2,1)S(1)}, u32[]{:S(2)}, u32[]{:S(2)}) async-start(bf16[8,72,1024]{2,1,0:T(8,128)(2,1)} %bitcast.152), calls=%async_computation.3 | async-start | bytes 2359296 | tf_op jit(solution)/shard_map/all_to_all | solution.py:126
  142.8 16.3 %all-to-all-done.3 = bf16[8,72,1024]{2,1,0:T(8,128)(2,1)S(1)} async-done(((bf16[8,72,1024]{2,1,0:T(8,128)(2,1)}), bf16[8,72,1024]{2,1,0:T(8,128)(2,1)S(1)}, u32[]{:S(2)}, u32[]{:S(2)}) %all-to-all-start.3) | async-done | bytes 1179680 | tf_op jit(solution)/shard_map/all_to_all | solution.py:126
  159.2 2.8 gather_fusion.1
  161.9 2.7 fusion.16
  164.7 2.0 add_add_fusion.1
  166.6 1.9 reduce_sum.384
  168.6 20.3 %multiply_reduce_fusion.30 = (f32[1024]{0:T(1024)S(1)}, f32[1024]{0:T(1024)S(1)}, f32[1024]{0:T(1024)S(1)}, f32[1024]{0:T(1024)S(1)}, f32[1024]{0:T(1024)S(1)}, ...) fusion(f32[2,256,1024]{2,1,0:T(8,128)} %copy-done.4, ...), kind=kLoop, calls=%fused_computation.98 | loop fusion | flops 27249664 | bytes 11610624 | tf_op jit(solution)/shard_map/transpose(jvp())/reduce_sum | solution.py:22
  188.9 4.9 %multiply_reduce_fusion.31 = (f32[1024]{0:T(1024)S(1)}, f32[1024]{0:T(1024)S(1)}, f32[1024]{0:T(1024)S(1)}, f32[1024]{0:T(1024)S(1)}, f32[1024]{0:T(1024)S(1)}, ...) fusion(f32[2,256,1024]{2,1,0:T(8,128)S(1)} %get-tuple-element.6, ...), kind=kLoop, calls=%fused_computation.99 | loop fusion | flops 18855936 | bytes 4268032 | tf_op jit(solution)/shard_map/transpose(jvp())/reduce_sum | solution.py:22
  194.1 9.2 %broadcast_multiply_fusion.1 = (f32[2,256,1024]{2,1,0:T(8,128)}, f32[2,256,1024]{2,1,0:T(8,128)}, f32[2,256,1024]{2,1,0:T(8,128)}, f32[2,256,1024]{2,1,0:T(8,128...) fusion(f32[2,256,1024]{2,1,0:T(8,128)S(1)} %get-tuple-element.6, ...), kind=kLoop, calls=%fused_computation.114 | loop fusion | flops 6815744 | bytes 29413376 | tf_op jit(solution)/shard_map/transpose(jvp())/mul | solution.py:22
  203.3 12.4 %broadcast_multiply_fusion = (f32[2,256,1024]{2,1,0:T(8,128)}, f32[2,256,1024]{2,1,0:T(8,128)}, f32[2,256,1024]{2,1,0:T(8,128)}, f32[2,256,1024]{2,1,0:T(8,128)}...) fusion(f32[2,256,1024]{2,1,0:T(8,128)S(1)} %get-tuple-element.6, ...), kind=kLoop, calls=%fused_computation.113 | loop fusion | flops 9437184 | bytes 39919616 | tf_op jit(solution)/shard_map/transpose(jvp())/mul | solution.py:22
  215.7 22.6 %pad_add_fusion = f32[2,286,1024]{2,1,0:T(8,128)} fusion(f32[2,256,1024]{2,1,0:T(8,128)} %get-tuple-element.76, f32[2,256,1024]{2,1,0:T(8,128)} %get-tuple-element.77, f32[2,256,1024]{2,1,0:T(8,128)} %get-tuple-element.78, f32[2,256,1024]{2,1,0:T(8,128)} %get-tuple-element.79, f32[2,256,1024]{2,1,0:T(8,128)} %get-tuple-element.80, ...), kind=kLoop, calls=%fused_computation.17 | loop fusion | flops 14057472 | bytes 54771712 | tf_op jit(solution)/shard_map/transpose(jvp())/add_any | solution.py:22
  238.3 6.9 %multiply_reduce_fusion.32 = (f32[2,256]{1,0:T(2,128)S(1)}, f32[2,256,1024]{2,1,0:T(8,128)S(1)}, f32[2,256,1024]{2,1,0:T(8,128)S(1)}) fusion(f32[1024]{0:T(1024)S(1)} %copy-done.9, f32[2,256]{1,0:T(2,128)S(1)} %div.56, bf16[2,256,1024]{2,1,0:T(8,128)(2,1)S(1)} %bitcast.146, f32[2,256]{1,0:T(2,128)S(1)} %get-tuple-element.133, ...), kind=kLoop, calls=%fused_computation.101 | loop fusion | flops 6290944 | bytes 19933184 | tf_op jit(solution)/shard_map/transpose(jvp())/reduce_sum | solution.py:11
  245.2 1.1 multiply_reduce_fusion
  246.5 1.1 collective-permute-start
  247.5 1.0 collective-permute-done
  249.1 5.1 %collective-permute-done.1 = f32[33,1024]{1,0:T(8,128)S(1)} collective-permute-done((f32[33,1024]{1,0:T(8,128)S(1)}, f32[33,1024]{1,0:T(8,128)S(1)}, u32[]{:S(2)}, u32[]{:S(2)}) %collective-permute-start.1) | collective-permute-done | bytes 135200 | tf_op jit(solution)/shard_map/ppermute | solution.py:50
  254.2 1.1 collective-permute-start.2
  255.3 4.9 %all-to-all-start.2 = ((bf16[8,72,1024]{2,1,0:T(8,128)(2,1)}), bf16[8,72,1024]{2,1,0:T(8,128)(2,1)S(1)}, u32[]{:S(2)}, u32[]{:S(2)}) async-start(bf16[8,72,1024]{2,1,0:T(8,128)(2,1)} %bitcast.151), calls=%async_computation.2 | async-start | bytes 2359296 | tf_op jit(solution)/shard_map/all_to_all | solution.py:119
  260.5 1.0 add.381
  261.5 1.4 collective-permute-start.3
  262.9 7.5 %collective-permute-done.3 = f32[33,1024]{1,0:T(8,128)S(1)} collective-permute-done((f32[33,1024]{1,0:T(8,128)S(1)}, f32[33,1024]{1,0:T(8,128)S(1)}, u32[]{:S(2)}, u32[]{:S(2)}) %collective-permute-start.3) | collective-permute-done | bytes 135200 | tf_op jit(solution)/shard_map/ppermute | solution.py:50
  270.4 3.2 collective-permute-start.4
  273.6 7.5 %collective-permute-done.4 = f32[33,1024]{1,0:T(8,128)S(1)} collective-permute-done((f32[33,1024]{1,0:T(8,128)S(1)}, f32[33,1024]{1,0:T(8,128)S(1)}, u32[]{:S(2)}, u32[]{:S(2)}) %collective-permute-start.4) | collective-permute-done | bytes 135200 | tf_op jit(solution)/shard_map/ppermute | solution.py:50
  281.1 1.5 collective-permute-start.5
  282.6 3.9 %add_convert_fusion = bf16[2,256,1024]{2,1,0:T(8,128)(2,1)} fusion(f32[2,256]{1,0:T(2,128)S(1)} %negate_multiply_fusion, f32[2,256]{1,0:T(2,128)S(1)} %negate_multiply_fusion.1, f32[2,256]{1,0:T(2,128)S(1)} %multiply_multiply_fusion.1, f32[2,256]{1,0:T(2,128)S(1)} %div.56, f32[2,256]{1,0:T(2,128)S(1)} %rsqrt.22, f32[2,256,1024]{2,1,0:T(8,128)} %copy-done.6, ...), kind=kLoop, calls=%fused_computation.100 | loop fusion | flops 11010048 | bytes 8413696 | tf_op jit(solution)/shard_map/convert_element_type | solution.py:164
  286.5 2.8 gather_fusion
  289.3 0.9 add.384
  290.2 2.9 collective-permute-start.6
  293.1 2.8 fusion.18
  295.9 3.7 %collective-permute-done.6 = f32[33,1024]{1,0:T(8,128)S(1)} collective-permute-done((f32[33,1024]{1,0:T(8,128)S(1)}, f32[33,1024]{1,0:T(8,128)S(1)}, u32[]{:S(2)}, u32[]{:S(2)}) %collective-permute-start.6) | collective-permute-done | bytes 135200 | tf_op jit(solution)/shard_map/ppermute | solution.py:50
  300.9 29.3 %reduce-scatter.3.cloned.1.call-done = f32[1024,256]{1,0:T(8,128)} async-done(((f32[1024,4096]{1,0:T(8,128)}), f32[1024,256]{1,0:T(8,128)}) %reduce-scatter.3.cloned.1.call-update) | async-done | bytes 1048592 | tf_op jit(solution)/shard_map/reduce_scatter | solution.py:116
  (77 shorter events, 6.1 us)
Async XLA Ops:
  7.9 7.4 %copy-start.13 = (pred[512]{0:T(512)(128)(4,1)}, pred[512]{0:T(512)(128)(4,1)S(1)}, u32[]{:S(2)}) copy-start(pred[512]{0:T(512)(128)(4,1)S(1)} %gt.26) | copy-start | bytes 1540
  10.8 11.4 %copy-start = (bf16[512,1024]{1,0:T(8,128)(2,1)S(1)}, bf16[512,1024]{1,0:T(8,128)(2,1)}, u32[]{:S(2)}) copy-start(bf16[512,1024]{1,0:T(8,128)(2,1)} %param.9) | copy-start | bytes 3145732
  15.3 7.6 %copy-start.8 = (f32[31,1024]{1,0:T(8,128)S(1)}, f32[31,1024]{1,0:T(8,128)}, u32[]{:S(2)}) copy-start(f32[31,1024]{1,0:T(8,128)} %param.12) | copy-start | bytes 380932
  15.3 7.8 %copy-start.9 = (f32[1024]{0:T(1024)S(1)}, f32[1024]{0:T(1024)}, u32[]{:S(2)}) copy-start(f32[1024]{0:T(1024)} %param.13) | copy-start | bytes 12292
  15.3 23.4 %all-to-all-start = ((bf16[8,72,1024]{2,1,0:T(8,128)(2,1)}), bf16[8,72,1024]{2,1,0:T(8,128)(2,1)}, u32[]{:S(2)}, u32[]{:S(2)}) async-start(bf16[8,72,1024]{2,1,0:T(8,128)(2,1)} %bitcast.39), calls=%async_computation | async-start | bytes 2359296 | tf_op jit(solution)/shard_map/all_to_all | solution.py:79
  22.3 278.6 %reduce-scatter.5.cloned.1.call-start = ((), (), s32[]{:S(2)}) async-start(), calls=%async_computation.7 | async-start | bytes 17825792 | tf_op jit(solution)/shard_map/reduce_scatter | solution.py:110
  23.1 10.0 %copy-start.11 = (f32[2,256]{1,0:T(2,128)}, f32[2,256]{1,0:T(2,128)S(1)}, u32[]{:S(2)}) copy-start(f32[2,256]{1,0:T(2,128)S(1)} %add.338) | copy-start | bytes 6148
  23.5 9.6 %copy-start.4 = (f32[2,256,1024]{2,1,0:T(8,128)}, f32[2,256,1024]{2,1,0:T(8,128)S(1)}, u32[]{:S(2)}) copy-start(f32[2,256,1024]{2,1,0:T(8,128)S(1)} %multiply_multiply_fusion) | copy-start | bytes 6291460
  33.1 0.7 copy-start.10
  81.6 2.2 copy-start.15
  95.4 234.8 %reduce-scatter.3.cloned.1.call-start = ((), (), s32[]{:S(2)}) async-start(), calls=%async_computation.6 | async-start | bytes 17825792 | tf_op jit(solution)/shard_map/reduce_scatter | solution.py:116
  105.9 2.1 copy-start.7
  138.1 21.1 %all-to-all-start.3 = ((bf16[8,72,1024]{2,1,0:T(8,128)(2,1)}), bf16[8,72,1024]{2,1,0:T(8,128)(2,1)S(1)}, u32[]{:S(2)}, u32[]{:S(2)}) async-start(bf16[8,72,1024]{2,1,0:T(8,128)(2,1)} %bitcast.152), calls=%async_computation.3 | async-start | bytes 2359296 | tf_op jit(solution)/shard_map/all_to_all | solution.py:126
  161.9 2.7 copy-start.3
  166.6 2.0 copy-start.1
  168.6 20.3 %copy-start.5 = (f32[2,256,1024]{2,1,0:T(8,128)S(1)}, f32[2,256,1024]{2,1,0:T(8,128)}, u32[]{:S(2)}) copy-start(f32[2,256,1024]{2,1,0:T(8,128)} %copy-done.4) | copy-start | bytes 6291460
  238.3 6.9 %copy-start.12 = (f32[2,256]{1,0:T(2,128)S(1)}, f32[2,256]{1,0:T(2,128)}, u32[]{:S(2)}) copy-start(f32[2,256]{1,0:T(2,128)} %copy-done.11) | copy-start | bytes 6148
  245.1 1.3 copy-start.6
  246.5 2.1 collective-permute-start
  248.6 5.6 %collective-permute-start.1 = (f32[33,1024]{1,0:T(8,128)S(1)}, f32[33,1024]{1,0:T(8,128)S(1)}, u32[]{:S(2)}, u32[]{:S(2)}) collective-permute-start(f32[33,1024]{1,0:T(8,128)S(1)} %fusion.39), channel_id=1, source_target_pairs={{0,2},{1,3},{2,0},{3,1},{4,6},{5,7},{6,4},{7,5},{8,10},{9,11},{10,... | collective-permute-start | bytes 405512 | tf_op jit(solution)/shard_map/ppermute | solution.py:50
  254.2 6.3 %collective-permute-start.2 = (f32[33,1024]{1,0:T(8,128)S(1)}, f32[33,1024]{1,0:T(8,128)}, u32[]{:S(2)}, u32[]{:S(2)}) collective-permute-start(f32[33,1024]{1,0:T(8,128)S(1)} %add.380), channel_id=1, source_target_pairs={{0,4},{1,5},{2,6},{3,7},{4,0},{5,1},{6,2},{7,3},{8,12},{9,13},{10,... | collective-permute-start | bytes 405512 | tf_op jit(solution)/shard_map/ppermute | solution.py:50
  255.3 31.2 %all-to-all-start.2 = ((bf16[8,72,1024]{2,1,0:T(8,128)(2,1)}), bf16[8,72,1024]{2,1,0:T(8,128)(2,1)S(1)}, u32[]{:S(2)}, u32[]{:S(2)}) async-start(bf16[8,72,1024]{2,1,0:T(8,128)(2,1)} %bitcast.151), calls=%async_computation.2 | async-start | bytes 2359296 | tf_op jit(solution)/shard_map/all_to_all | solution.py:119
  260.2 22.3 %copy-start.2 = (bf16[512,1024]{1,0:T(8,128)(2,1)S(1)}, bf16[512,1024]{1,0:T(8,128)(2,1)}, u32[]{:S(2)}) copy-start(bf16[512,1024]{1,0:T(8,128)(2,1)} %param.9) | copy-start | bytes 3145732
  261.5 8.9 %collective-permute-start.3 = (f32[33,1024]{1,0:T(8,128)S(1)}, f32[33,1024]{1,0:T(8,128)S(1)}, u32[]{:S(2)}, u32[]{:S(2)}) collective-permute-start(f32[33,1024]{1,0:T(8,128)S(1)} %add.381), channel_id=1, source_target_pairs={{0,8},{8,0},{16,24},{24,16},{32,40},{40,32},{48,56},{56,48},{64,72... | collective-permute-start | bytes 405512 | tf_op jit(solution)/shard_map/ppermute | solution.py:50
  270.4 10.6 %collective-permute-start.4 = (f32[33,1024]{1,0:T(8,128)S(1)}, f32[33,1024]{1,0:T(8,128)S(1)}, u32[]{:S(2)}, u32[]{:S(2)}) collective-permute-start(f32[33,1024]{1,0:T(8,128)S(1)} %add.382), channel_id=1, source_target_pairs={{0,16},{8,24},{16,0},{24,8},{32,48},{40,56},{48,32},{56,40},{64,80... | collective-permute-start | bytes 405512 | tf_op jit(solution)/shard_map/ppermute | solution.py:50
  281.1 8.2 %collective-permute-start.5 = (f32[33,1024]{1,0:T(8,128)S(1)}, f32[33,1024]{1,0:T(8,128)}, u32[]{:S(2)}, u32[]{:S(2)}) collective-permute-start(f32[33,1024]{1,0:T(8,128)S(1)} %add.383), channel_id=1, source_target_pairs={{0,32},{8,40},{16,48},{24,56},{32,0},{40,8},{48,16},{56,24},{64,96... | collective-permute-start | bytes 405512 | tf_op jit(solution)/shard_map/ppermute | solution.py:50
  286.5 6.6 %copy-start.14 = (pred[512]{0:T(512)(128)(4,1)S(1)}, pred[512]{0:T(512)(128)(4,1)}, u32[]{:S(2)}) copy-start(pred[512]{0:T(512)(128)(4,1)} %copy-done.13) | copy-start | bytes 1540
  290.2 9.4 %collective-permute-start.6 = (f32[33,1024]{1,0:T(8,128)S(1)}, f32[33,1024]{1,0:T(8,128)S(1)}, u32[]{:S(2)}, u32[]{:S(2)}) collective-permute-start(f32[33,1024]{1,0:T(8,128)S(1)} %add.384), channel_id=1, source_target_pairs={{0,64},{8,72},{16,80},{24,88},{32,96},{40,104},{48,112},{56,120},{... | collective-permute-start | bytes 405512 | tf_op jit(solution)/shard_map/ppermute | solution.py:50
Sparse Core Ops, SparseCore 0:
  95.5 109.9 reduce-scatter.4
  209.4 120.6 reduce-scatter.2

commit v4 on v3

--- a/solution.py
+++ b/solution.py
@@ -111,9 +111,9 @@
     out_rows = jnp.dot(hidden, weights_out, preferred_element_type=jnp.float32).astype(jnp.bfloat16)
     hidden_grad = times_transpose(grad_rows, weights_out)
     pre_grad = (hidden_grad * silu_slope(pre_act)).astype(jnp.bfloat16)
-    full_in = contract_rows(routed_in, pre_grad)
-    full_in, out_rows, pre_grad = lax.optimization_barrier((full_in, out_rows, pre_grad))
-    grad_in = lax.psum_scatter(full_in, "dp", scatter_dimension=1, tiled=True)
+    full_in_t = contract_rows(pre_grad, routed_in)
+    full_in_t, out_rows, pre_grad = lax.optimization_barrier((full_in_t, out_rows, pre_grad))
+    grad_in = lax.psum_scatter(full_in_t, "dp", scatter_dimension=0, tiled=True).T
     back_rows = times_transpose(pre_grad, weights_in).astype(jnp.bfloat16)
     ret_out, ret_back = (
         lax.all_to_all(

time: 340 us -> 374 us (1.10)
  waiting for transfers between devices: 71.8 us -> 104 us
    reduce_scatter x1, waiting for transfers between devices: 0.01 us -> 61.1 us  [shards(): grad_out = lax.psum_scatter(full_out, 'dp', scatter_dimension=0, tiled=True)]
    reduce_scatter x1, waiting for transfers between devices: 29.3 us -> 0.01 us  [shards(): lax.psum_scatter(full_in_t, 'dp', scatter_dimension=0, tiled=True)]
  transfers between devices with their start and end apart: 12 -> 12, of which waited for: 9 -> 7; matrix products, arithmetic and copies ran while one was open for 46% -> 34% of each run, Pallas kernels for 0% -> 0%
where the time goes in v4:
time: 374 us; the launch traced here: 372 us
  other arithmetic  112 us (30%)
  waiting for transfers between devices  104 us (28%)
  matrix products  62.3 us (17%)
  blocking collectives  32.1 us (9%)
  starting transfers between devices  28.5 us (8%)
  local copies, waits for them, and re-layouts  18.1 us (5%)
  between operations  14.5 us (4%)
    reduce_scatter x1, waiting for transfers between devices, shards(): grad_out = lax.psum_scatter(full_out, 'dp', scatter_dimension=0, tiled=True)  61.1 us
    all_to_all x1, blocking collectives, shards(): lax.all_to_all(send_in.reshape(expert_count, capacity, feat_width), 'expe...  32.1 us
    ppermute x7, waiting for transfers between devices, butterfly_sum(): values = values + lax.ppermute(values, axis_name, pairs)  25.4 us
    reduce_sum x2, other arithmetic, conv_module(): conv_kernel[tap_index] * padded[:, tap_index:tap_index + utt_len]  24.9 us
    add_any x1, other arithmetic, conv_module(): padded[:, tap_index:tap_index + utt_len]  22.5 us
    dot_general x2, matrix products, contract_rows(): lax.dot_general(left_rows, right_rows, (((0,), (0,)), ((), ())), preferre...  21.8 us
    mul x2, other arithmetic, conv_module(): conv_kernel[tap_index] * padded[:, tap_index:tap_index + utt_len]  21.6 us
    dot_general x2, matrix products, times_transpose(): lax.dot_general(left_rows, matrix, (((1,), (1,)), ((), ())), preferred_el...  19.2 us
  transfers between devices with their start and end apart: 12, of which 7 were waited for; matrix products, arithmetic and copies ran while one was open for 34% of the time, Pallas kernels for 0%

profile of v4, /device:TPU:1, one launch (start us, length us, event | category | flops | bytes accessed | tf_op | source)
XLA Modules:
  0.0 371.5 jit_solution(1718758465914676440)
XLA Ops:
  8.6 1.1 reduce-window.6
  10.8 4.5 %scatter_custom_fusion = bf16[576,1024]{1,0:T(8,128)(2,1)} fusion(s32[512]{0:T(512)S(1)} %bitcast.261, bf16[512,1024]{1,0:T(8,128)(2,1)} %param.17, pred[512]{0:T(512)(128)(4,1)S(1)} %gt.26, bf16[]{:T(256)} %constant.44.clone.1), kind=kCustom, calls=%fused_computation.111 | custom fusion | flops 524288 | bytes 2229760 | tf_op jit(solution)/shard_map/scatter | solution.py:77
  15.3 6.9 %all-to-all-start = ((bf16[8,72,1024]{2,1,0:T(8,128)(2,1)}), bf16[8,72,1024]{2,1,0:T(8,128)(2,1)}, u32[]{:S(2)}, u32[]{:S(2)}) async-start(bf16[8,72,1024]{2,1,0:T(8,128)(2,1)} %bitcast.39), calls=%async_computation | async-start | bytes 2359296 | tf_op jit(solution)/shard_map/all_to_all | solution.py:79
  23.5 9.6 %multiply_add_fusion = (f32[2,256,1024]{2,1,0:T(8,128)S(1)}, f32[2,256,1024]{2,1,0:T(8,128)}) fusion(f32[2,256]{1,0:T(2,128)S(1)} %get-tuple-element.145, bf16[512,1024]{1,0:T(8,128)(2,1)S(1)} %copy-done, f32[1024]{0:T(1024)S(1)} %bitcast.208, f32[1024]{0:T(1024)S(1)} %bitcast.162, f32[1024]{0:T(1024)S(1)} %bitcast.164, f32[1024]{0:T(1024)S(1)} %bitcast.166, ...), kind=kLoop, calls=%fused_computation.104 | loop fusion | flops 35651584 | bytes 7469056 | tf_op jit(solution)/shard_map/add | solution.py:23
  33.9 1.3 multiply_convert_fusion.2
  35.2 3.5 scatter_custom_fusion.1
  38.7 32.1 %all_to_all.20 = bf16[8,72,1024]{2,1,0:T(8,128)(2,1)S(1)} all-to-all(bf16[8,72,1024]{2,1,0:T(8,128)(2,1)S(1)} %bitcast.150), channel_id=1, replica_groups=mesh['dp'=16,'expert'=8] {'expert'}, dimensions={0} | all-to-all | bytes 2359296 | tf_op jit(solution)/shard_map/all_to_all | solution.py:93
  70.8 11.6 %multiply_convert_fusion.1 = (bf16[576,4096]{1,0:T(8,128)(2,1)S(1)}, f32[576,4096]{1,0:T(8,128)}) fusion(bf16[576,1024]{1,0:T(8,128)(2,1)S(1)} %bitcast.152, bf16[1,1024,4096]{2,1,0:T(8,128)(2,1)} %param.15), kind=kOutput, calls=%fused_computation.5 | convolution fusion | flops 4843634688 | bytes 23724032 | tf_op jit(solution)/shard_map/dot_general | solution.py:104
  82.4 2.2 copy-done.17
  84.6 11.5 %fusion.44 = f32[4096,1024]{1,0:T(8,128)} fusion(bf16[576,4096]{1,0:T(8,128)(2,1)S(1)} %get-tuple-element.21, bf16[576,1024]{1,0:T(8,128)(2,1)} %bitcast.44), kind=kOutput, calls=%fused_computation.179 | convolution fusion | flops 4831838208 | bytes 22675456 | tf_op jit(solution)/shard_map/dot_general | solution.py:33
  96.1 9.8 %fusion.24 = bf16[576,1024]{1,0:T(8,128)(2,1)} fusion(bf16[576,4096]{1,0:T(8,128)(2,1)} %copy-done.17, bf16[1,4096,1024]{2,1,0:T(8,128)(2,1)} %param.16), kind=kOutput, calls=%fused_computation.110 | convolution fusion | flops 4832428032 | bytes 14286848 | tf_op jit(solution)/shard_map/dot_general | solution.py:111
  105.9 9.4 %multiply_convert_fusion = bf16[576,4096]{1,0:T(8,128)(2,1)S(1)} fusion(f32[576,4096]{1,0:T(8,128)S(1)} %copy-done.18, bf16[576,1024]{1,0:T(8,128)(2,1)} %bitcast.44, bf16[1,4096,1024]{2,1,0:T(8,128)(2,1)} %param.16), kind=kOutput, calls=%fused_computation.4 | convolution fusion | flops 4853071872 | bytes 23724032 | tf_op jit(solution)/shard_map/dot_general | solution.py:39
  115.3 2.2 copy-done.16
  117.6 10.3 %fusion.45 = f32[4096,1024]{1,0:T(8,128)} fusion(bf16[576,4096]{1,0:T(8,128)(2,1)S(1)} %multiply_convert_fusion, bf16[576,1024]{1,0:T(8,128)(2,1)S(1)} %bitcast.153), kind=kOutput, calls=%fused_computation.180 | convolution fusion | flops 4831838208 | bytes 22675456 | tf_op jit(solution)/shard_map/dot_general | solution.py:33
  128.6 9.8 %fusion.21 = bf16[576,1024]{1,0:T(8,128)(2,1)} fusion(bf16[576,4096]{1,0:T(8,128)(2,1)} %copy-done.16, bf16[1,1024,4096]{2,1,0:T(8,128)(2,1)} %param.15), kind=kOutput, calls=%fused_computation.109 | convolution fusion | flops 4832428032 | bytes 14286848 | tf_op jit(solution)/shard_map/dot_general | solution.py:39
  138.4 4.8 %all-to-all-start.3 = ((bf16[8,72,1024]{2,1,0:T(8,128)(2,1)}), bf16[8,72,1024]{2,1,0:T(8,128)(2,1)S(1)}, u32[]{:S(2)}, u32[]{:S(2)}) async-start(bf16[8,72,1024]{2,1,0:T(8,128)(2,1)} %bitcast.154), calls=%async_computation.3 | async-start | bytes 2359296 | tf_op jit(solution)/shard_map/all_to_all | solution.py:126
  143.2 16.3 %all-to-all-done.3 = bf16[8,72,1024]{2,1,0:T(8,128)(2,1)S(1)} async-done(((bf16[8,72,1024]{2,1,0:T(8,128)(2,1)}), bf16[8,72,1024]{2,1,0:T(8,128)(2,1)S(1)}, u32[]{:S(2)}, u32[]{:S(2)}) %all-to-all-start.3) | async-done | bytes 1179680 | tf_op jit(solution)/shard_map/all_to_all | solution.py:126
  159.5 2.8 gather_fusion.1
  162.3 2.7 fusion.16
  165.0 2.0 add_add_fusion.1
  167.0 1.9 reduce_sum.384
  168.8 20.0 %multiply_reduce_fusion.30 = (f32[1024]{0:T(1024)S(1)}, f32[1024]{0:T(1024)S(1)}, f32[1024]{0:T(1024)S(1)}, f32[1024]{0:T(1024)S(1)}, f32[1024]{0:T(1024)S(1)}, ...) fusion(f32[2,256,1024]{2,1,0:T(8,128)} %copy-done.4, ...), kind=kLoop, calls=%fused_computation.98 | loop fusion | flops 27249664 | bytes 11610624 | tf_op jit(solution)/shard_map/transpose(jvp())/reduce_sum | solution.py:22
  188.9 4.9 %multiply_reduce_fusion.31 = (f32[1024]{0:T(1024)S(1)}, f32[1024]{0:T(1024)S(1)}, f32[1024]{0:T(1024)S(1)}, f32[1024]{0:T(1024)S(1)}, f32[1024]{0:T(1024)S(1)}, ...) fusion(f32[2,256,1024]{2,1,0:T(8,128)S(1)} %get-tuple-element.7, ...), kind=kLoop, calls=%fused_computation.99 | loop fusion | flops 18855936 | bytes 4268032 | tf_op jit(solution)/shard_map/transpose(jvp())/reduce_sum | solution.py:22
  194.0 9.2 %broadcast_multiply_fusion.1 = (f32[2,256,1024]{2,1,0:T(8,128)}, f32[2,256,1024]{2,1,0:T(8,128)}, f32[2,256,1024]{2,1,0:T(8,128)}, f32[2,256,1024]{2,1,0:T(8,128...) fusion(f32[2,256,1024]{2,1,0:T(8,128)S(1)} %get-tuple-element.7, ...), kind=kLoop, calls=%fused_computation.114 | loop fusion | flops 6815744 | bytes 29413376 | tf_op jit(solution)/shard_map/transpose(jvp())/mul | solution.py:22
  203.3 12.4 %broadcast_multiply_fusion = (f32[2,256,1024]{2,1,0:T(8,128)}, f32[2,256,1024]{2,1,0:T(8,128)}, f32[2,256,1024]{2,1,0:T(8,128)}, f32[2,256,1024]{2,1,0:T(8,128)}...) fusion(f32[2,256,1024]{2,1,0:T(8,128)S(1)} %get-tuple-element.7, ...), kind=kLoop, calls=%fused_computation.113 | loop fusion | flops 9437184 | bytes 39919616 | tf_op jit(solution)/shard_map/transpose(jvp())/mul | solution.py:22
  215.6 22.5 %pad_add_fusion = f32[2,286,1024]{2,1,0:T(8,128)} fusion(f32[2,256,1024]{2,1,0:T(8,128)} %get-tuple-element.88, f32[2,256,1024]{2,1,0:T(8,128)} %get-tuple-element.89, f32[2,256,1024]{2,1,0:T(8,128)} %get-tuple-element.90, f32[2,256,1024]{2,1,0:T(8,128)} %get-tuple-element.91, f32[2,256,1024]{2,1,0:T(8,128)} %get-tuple-element.92, ...), kind=kLoop, calls=%fused_computation.17 | loop fusion | flops 14057472 | bytes 54771712 | tf_op jit(solution)/shard_map/transpose(jvp())/add_any | solution.py:22
  238.2 6.2 %multiply_reduce_fusion.32 = (f32[2,256]{1,0:T(2,128)S(1)}, f32[2,256,1024]{2,1,0:T(8,128)S(1)}, f32[2,256,1024]{2,1,0:T(8,128)S(1)}) fusion(f32[1024]{0:T(1024)S(1)} %copy-done.10, f32[2,256]{1,0:T(2,128)S(1)} %div.56, bf16[2,256,1024]{2,1,0:T(8,128)(2,1)S(1)} %bitcast.148, f32[2,256]{1,0:T(2,128)S(1)} %get-tuple-element.145, ...), kind=kLoop, calls=%fused_computation.101 | loop fusion | flops 6290944 | bytes 19933184 | tf_op jit(solution)/shard_map/transpose(jvp())/reduce_sum | solution.py:11
  244.5 1.1 multiply_reduce_fusion
  245.8 0.8 collective-permute-start
  246.6 1.0 collective-permute-done
  247.6 0.8 collective-permute-start.1
  248.4 4.7 %collective-permute-done.1 = f32[33,1024]{1,0:T(8,128)S(1)} collective-permute-done((f32[33,1024]{1,0:T(8,128)S(1)}, f32[33,1024]{1,0:T(8,128)S(1)}, u32[]{:S(2)}, u32[]{:S(2)}) %collective-permute-start.1) | collective-permute-done | bytes 135200 | tf_op jit(solution)/shard_map/ppermute | solution.py:50
  253.1 1.5 collective-permute-start.2
  254.7 4.7 %all-to-all-start.2 = ((bf16[8,72,1024]{2,1,0:T(8,128)(2,1)}), bf16[8,72,1024]{2,1,0:T(8,128)(2,1)S(1)}, u32[]{:S(2)}, u32[]{:S(2)}) async-start(bf16[8,72,1024]{2,1,0:T(8,128)(2,1)} %bitcast.151), calls=%async_computation.2 | async-start | bytes 2359296 | tf_op jit(solution)/shard_map/all_to_all | solution.py:119
  259.4 1.0 add.381
  260.4 1.5 collective-permute-start.3
  261.9 7.3 %collective-permute-done.3 = f32[33,1024]{1,0:T(8,128)S(1)} collective-permute-done((f32[33,1024]{1,0:T(8,128)S(1)}, f32[33,1024]{1,0:T(8,128)S(1)}, u32[]{:S(2)}, u32[]{:S(2)}) %collective-permute-start.3) | collective-permute-done | bytes 135200 | tf_op jit(solution)/shard_map/ppermute | solution.py:50
  269.3 3.3 collective-permute-start.4
  272.6 7.4 %collective-permute-done.4 = f32[33,1024]{1,0:T(8,128)S(1)} collective-permute-done((f32[33,1024]{1,0:T(8,128)S(1)}, f32[33,1024]{1,0:T(8,128)S(1)}, u32[]{:S(2)}, u32[]{:S(2)}) %collective-permute-start.4) | collective-permute-done | bytes 135200 | tf_op jit(solution)/shard_map/ppermute | solution.py:50
  280.0 1.6 collective-permute-start.5
  281.6 3.9 %add_convert_fusion = bf16[2,256,1024]{2,1,0:T(8,128)(2,1)} fusion(f32[2,256]{1,0:T(2,128)S(1)} %negate_multiply_fusion, f32[2,256]{1,0:T(2,128)S(1)} %negate_multiply_fusion.1, f32[2,256]{1,0:T(2,128)S(1)} %multiply_multiply_fusion.1, f32[2,256]{1,0:T(2,128)S(1)} %div.56, f32[2,256]{1,0:T(2,128)S(1)} %rsqrt.22, f32[2,256,1024]{2,1,0:T(8,128)} %copy-done.6, ...), kind=kLoop, calls=%fused_computation.100 | loop fusion | flops 11010048 | bytes 8413696 | tf_op jit(solution)/shard_map/convert_element_type | solution.py:164
  285.5 2.8 gather_fusion
  288.3 0.9 add.384
  289.2 2.5 collective-permute-start.6
  291.8 2.8 fusion.18
  294.6 5.0 %collective-permute-done.6 = f32[33,1024]{1,0:T(8,128)S(1)} collective-permute-done((f32[33,1024]{1,0:T(8,128)S(1)}, f32[33,1024]{1,0:T(8,128)S(1)}, u32[]{:S(2)}, u32[]{:S(2)}) %collective-permute-start.6) | collective-permute-done | bytes 135200 | tf_op jit(solution)/shard_map/ppermute | solution.py:50
  300.9 2.6 copy.16
  303.4 61.1 %reduce-scatter.5.cloned.1.call-done = f32[256,1024]{1,0:T(8,128)} async-done(((f32[4096,1024]{1,0:T(8,128)}), f32[256,1024]{1,0:T(8,128)}) %reduce-scatter.5.cloned.1.call-update) | async-done | bytes 1048592 | tf_op jit(solution)/shard_map/reduce_scatter | solution.py:110
  (84 shorter events, 7.1 us)
Async XLA Ops:
  7.9 7.4 %copy-start.14 = (pred[512]{0:T(512)(128)(4,1)}, pred[512]{0:T(512)(128)(4,1)S(1)}, u32[]{:S(2)}) copy-start(pred[512]{0:T(512)(128)(4,1)S(1)} %gt.26) | copy-start | bytes 1540
  10.8 11.4 %copy-start = (bf16[512,1024]{1,0:T(8,128)(2,1)S(1)}, bf16[512,1024]{1,0:T(8,128)(2,1)}, u32[]{:S(2)}) copy-start(bf16[512,1024]{1,0:T(8,128)(2,1)} %param.9) | copy-start | bytes 3145732
  15.3 7.6 %copy-start.9 = (f32[31,1024]{1,0:T(8,128)S(1)}, f32[31,1024]{1,0:T(8,128)}, u32[]{:S(2)}) copy-start(f32[31,1024]{1,0:T(8,128)} %param.12) | copy-start | bytes 380932
  15.3 7.8 %copy-start.10 = (f32[1024]{0:T(1024)S(1)}, f32[1024]{0:T(1024)}, u32[]{:S(2)}) copy-start(f32[1024]{0:T(1024)} %param.13) | copy-start | bytes 12292
  15.3 23.4 %all-to-all-start = ((bf16[8,72,1024]{2,1,0:T(8,128)(2,1)}), bf16[8,72,1024]{2,1,0:T(8,128)(2,1)}, u32[]{:S(2)}, u32[]{:S(2)}) async-start(bf16[8,72,1024]{2,1,0:T(8,128)(2,1)} %bitcast.39), calls=%async_computation | async-start | bytes 2359296 | tf_op jit(solution)/shard_map/all_to_all | solution.py:79
  22.3 278.6 %reduce-scatter.3.cloned.1.call-start = ((), (), s32[]{:S(2)}) async-start(), calls=%async_computation.6 | async-start | bytes 17825792 | tf_op jit(solution)/shard_map/reduce_scatter | solution.py:116
  23.1 10.1 %copy-start.12 = (f32[2,256]{1,0:T(2,128)}, f32[2,256]{1,0:T(2,128)S(1)}, u32[]{:S(2)}) copy-start(f32[2,256]{1,0:T(2,128)S(1)} %add.338) | copy-start | bytes 6148
  23.5 9.6 %copy-start.4 = (f32[2,256,1024]{2,1,0:T(8,128)}, f32[2,256,1024]{2,1,0:T(8,128)S(1)}, u32[]{:S(2)}) copy-start(f32[2,256,1024]{2,1,0:T(8,128)S(1)} %multiply_multiply_fusion) | copy-start | bytes 6291460
  33.2 0.7 copy-start.11
  70.8 11.6 %copy-start.7 = (bf16[8,72,1024]{2,1,0:T(8,128)(2,1)}, bf16[8,72,1024]{2,1,0:T(8,128)(2,1)S(1)}, u32[]{:S(2)}) copy-start(bf16[8,72,1024]{2,1,0:T(8,128)(2,1)S(1)} %all_to_all.20) | copy-start | bytes 3538948
  82.4 2.2 copy-start.17
  96.1 9.8 %copy-start.18 = (f32[576,4096]{1,0:T(8,128)S(1)}, f32[576,4096]{1,0:T(8,128)}, u32[]{:S(2)}) copy-start(f32[576,4096]{1,0:T(8,128)} %get-tuple-element.19) | copy-start | bytes 28311556
  105.9 11.6 %copy-start.8 = (bf16[8,72,1024]{2,1,0:T(8,128)(2,1)S(1)}, bf16[8,72,1024]{2,1,0:T(8,128)(2,1)}, u32[]{:S(2)}) copy-start(bf16[8,72,1024]{2,1,0:T(8,128)(2,1)} %copy-done.7) | copy-start | bytes 3538948
  115.3 2.2 copy-start.16
  127.8 236.6 %reduce-scatter.5.cloned.1.call-start = ((), (), s32[]{:S(2)}) async-start(), calls=%async_computation.7 | async-start | bytes 17825792 | tf_op jit(solution)/shard_map/reduce_scatter | solution.py:110
  138.4 21.1 %all-to-all-start.3 = ((bf16[8,72,1024]{2,1,0:T(8,128)(2,1)}), bf16[8,72,1024]{2,1,0:T(8,128)(2,1)S(1)}, u32[]{:S(2)}, u32[]{:S(2)}) async-start(bf16[8,72,1024]{2,1,0:T(8,128)(2,1)} %bitcast.154), calls=%async_computation.3 | async-start | bytes 2359296 | tf_op jit(solution)/shard_map/all_to_all | solution.py:126
  162.3 2.7 copy-start.3
  167.0 1.9 copy-start.1
  168.8 20.1 %copy-start.5 = (f32[2,256,1024]{2,1,0:T(8,128)S(1)}, f32[2,256,1024]{2,1,0:T(8,128)}, u32[]{:S(2)}) copy-start(f32[2,256,1024]{2,1,0:T(8,128)} %copy-done.4) | copy-start | bytes 6291460
  238.2 6.3 %copy-start.13 = (f32[2,256]{1,0:T(2,128)S(1)}, f32[2,256]{1,0:T(2,128)}, u32[]{:S(2)}) copy-start(f32[2,256]{1,0:T(2,128)} %copy-done.12) | copy-start | bytes 6148
  244.4 1.3 copy-start.6
  245.8 1.8 collective-permute-start
  247.6 5.5 %collective-permute-start.1 = (f32[33,1024]{1,0:T(8,128)S(1)}, f32[33,1024]{1,0:T(8,128)S(1)}, u32[]{:S(2)}, u32[]{:S(2)}) collective-permute-start(f32[33,1024]{1,0:T(8,128)S(1)} %fusion.39), channel_id=1, source_target_pairs={{0,2},{1,3},{2,0},{3,1},{4,6},{5,7},{6,4},{7,5},{8,10},{9,11},{10,... | collective-permute-start | bytes 405512 | tf_op jit(solution)/shard_map/ppermute | solution.py:50
  253.1 6.2 %collective-permute-start.2 = (f32[33,1024]{1,0:T(8,128)S(1)}, f32[33,1024]{1,0:T(8,128)}, u32[]{:S(2)}, u32[]{:S(2)}) collective-permute-start(f32[33,1024]{1,0:T(8,128)S(1)} %add.380), channel_id=1, source_target_pairs={{0,4},{1,5},{2,6},{3,7},{4,0},{5,1},{6,2},{7,3},{8,12},{9,13},{10,... | collective-permute-start | bytes 405512 | tf_op jit(solution)/shard_map/ppermute | solution.py:50
  254.7 30.9 %all-to-all-start.2 = ((bf16[8,72,1024]{2,1,0:T(8,128)(2,1)}), bf16[8,72,1024]{2,1,0:T(8,128)(2,1)S(1)}, u32[]{:S(2)}, u32[]{:S(2)}) async-start(bf16[8,72,1024]{2,1,0:T(8,128)(2,1)} %bitcast.151), calls=%async_computation.2 | async-start | bytes 2359296 | tf_op jit(solution)/shard_map/all_to_all | solution.py:119
  259.4 22.2 %copy-start.2 = (bf16[512,1024]{1,0:T(8,128)(2,1)S(1)}, bf16[512,1024]{1,0:T(8,128)(2,1)}, u32[]{:S(2)}) copy-start(bf16[512,1024]{1,0:T(8,128)(2,1)} %param.9) | copy-start | bytes 3145732
  260.4 8.9 %collective-permute-start.3 = (f32[33,1024]{1,0:T(8,128)S(1)}, f32[33,1024]{1,0:T(8,128)S(1)}, u32[]{:S(2)}, u32[]{:S(2)}) collective-permute-start(f32[33,1024]{1,0:T(8,128)S(1)} %add.381), channel_id=1, source_target_pairs={{0,8},{8,0},{16,24},{24,16},{32,40},{40,32},{48,56},{56,48},{64,72... | collective-permute-start | bytes 405512 | tf_op jit(solution)/shard_map/ppermute | solution.py:50
  269.3 10.6 %collective-permute-start.4 = (f32[33,1024]{1,0:T(8,128)S(1)}, f32[33,1024]{1,0:T(8,128)S(1)}, u32[]{:S(2)}, u32[]{:S(2)}) collective-permute-start(f32[33,1024]{1,0:T(8,128)S(1)} %add.382), channel_id=1, source_target_pairs={{0,16},{8,24},{16,0},{24,8},{32,48},{40,56},{48,32},{56,40},{64,80... | collective-permute-start | bytes 405512 | tf_op jit(solution)/shard_map/ppermute | solution.py:50
  280.0 8.3 %collective-permute-start.5 = (f32[33,1024]{1,0:T(8,128)S(1)}, f32[33,1024]{1,0:T(8,128)}, u32[]{:S(2)}, u32[]{:S(2)}) collective-permute-start(f32[33,1024]{1,0:T(8,128)S(1)} %add.383), channel_id=1, source_target_pairs={{0,32},{8,40},{16,48},{24,56},{32,0},{40,8},{48,16},{56,24},{64,96... | collective-permute-start | bytes 405512 | tf_op jit(solution)/shard_map/ppermute | solution.py:50
  285.5 6.2 %copy-start.15 = (pred[512]{0:T(512)(128)(4,1)S(1)}, pred[512]{0:T(512)(128)(4,1)}, u32[]{:S(2)}) copy-start(pred[512]{0:T(512)(128)(4,1)} %copy-done.14) | copy-start | bytes 1540
  289.2 10.3 %collective-permute-start.6 = (f32[33,1024]{1,0:T(8,128)S(1)}, f32[33,1024]{1,0:T(8,128)S(1)}, u32[]{:S(2)}, u32[]{:S(2)}) collective-permute-start(f32[33,1024]{1,0:T(8,128)S(1)} %add.384), channel_id=1, source_target_pairs={{0,64},{8,72},{16,80},{24,88},{32,96},{40,104},{48,112},{56,120},{... | collective-permute-start | bytes 405512 | tf_op jit(solution)/shard_map/ppermute | solution.py:50
Sparse Core Ops, SparseCore 0:
  128.0 109.9 reduce-scatter.2
  242.0 122.4 reduce-scatter.4

commit v5 on v3

--- a/solution.py
+++ b/solution.py
@@ -71,11 +71,14 @@
     rank_in = jnp.sum((jnp.cumsum(one_hot, axis=0, dtype=jnp.int32) - 1) * one_hot, axis=1)
     dest_slot = jnp.where(live_flat, target * capacity + rank_in, slot_total)
     routed_grad = jnp.where(live_flat[:, None], out_grad, jnp.zeros_like(out_grad))
-    send_grad = (
-        jnp.zeros((slot_total, feat_width), jnp.bfloat16)
+    slot_src = (
+        jnp.full((slot_total,), frame_count, jnp.int32)
         .at[dest_slot]
-        .set(routed_grad, mode="drop")
+        .set(jnp.arange(frame_count, dtype=jnp.int32), mode="drop")
     )
+    slot_used = (slot_src < frame_count)[:, None]
+    slot_row = jnp.minimum(slot_src, frame_count - 1)
+    send_grad = jnp.where(slot_used, routed_grad[slot_row], jnp.zeros((), jnp.bfloat16))
     recv_grad = lax.all_to_all(
         send_grad.reshape(expert_count, capacity, feat_width),
         "expert",
@@ -86,9 +89,7 @@
     frames_f = frames.astype(jnp.float32).reshape(utt_count, utt_len, feat_width)
     residual, normed = conv_module(frames_f, live_mask, conv_kernel, conv_gain, ffn_gain)
     expert_in = normed.reshape(frame_count, feat_width).astype(jnp.bfloat16)
-    send_in = (
-        jnp.zeros((slot_total, feat_width), jnp.bfloat16).at[dest_slot].set(expert_in, mode="drop")
-    )
+    send_in = jnp.where(slot_used, expert_in[slot_row], jnp.zeros((), jnp.bfloat16))
     recv_grad, send_in = lax.optimization_barrier((recv_grad, send_in))
     recv_in = lax.all_to_all(
         send_in.reshape(expert_count, capacity, feat_width),

time: 340 us -> 340 us (level); the launches traced: 337 us -> 333 us
  blocking collectives: 31.8 us -> 21.8 us
  local copies, waits for them, and re-layouts: 15.5 us -> 21.3 us
    all_to_all x1, blocking collectives: 31.8 us -> 21.8 us  [shards(): lax.all_to_all(send_in.reshape(expert_count, capacity, feat_width), 'expe...]
    gather x0 -> x2, local copies, waits for them, and re-layouts: none -> 6.79 us  [the longest x1 3.4 us: shards(): routed_grad[slot_row]]
    select_n x1 -> x5, other arithmetic: 0.01 us -> 6.35 us  [the longest x1 2.55 us: shards(): jnp.where(slot_used, routed_grad[slot_row], jnp.zeros((), jnp.bfloat16))]
    scatter x1 -> x0, other arithmetic: 4.47 us -> none  [shards(): send_grad = jnp.zeros((slot_total, feat_width), jnp.bfloat16).at[dest_slo...]
  transfers between devices with their start and end apart: 12 -> 12, of which waited for: 9 -> 8; matrix products, arithmetic and copies ran while one was open for 46% -> 47% of each run, Pallas kernels for 0% -> 0%
where the time goes in v5:
time: 340 us; the launch traced here: 333 us
  other arithmetic  114 us (34%)
  waiting for transfers between devices  70.1 us (21%)
  matrix products  63.1 us (19%)
  starting transfers between devices  28.2 us (8%)
  blocking collectives  21.8 us (6%)
  local copies, waits for them, and re-layouts  21.3 us (6%)
  between operations  14.8 us (4%)
    reduce_scatter x1, waiting for transfers between devices, shards(): grad_in = lax.psum_scatter(full_in, 'dp', scatter_dimension=1, tiled=True)  29 us
    reduce_sum x2, other arithmetic, conv_module(): conv_kernel[tap_index] * padded[:, tap_index:tap_index + utt_len]  25.2 us
    ppermute x7, waiting for transfers between devices, butterfly_sum(): values = values + lax.ppermute(values, axis_name, pairs)  24.7 us
    add_any x1, other arithmetic, conv_module(): padded[:, tap_index:tap_index + utt_len]  22.7 us
    all_to_all x1, blocking collectives, shards(): lax.all_to_all(send_in.reshape(expert_count, capacity, feat_width), 'expe...  21.8 us
    dot_general x2, matrix products, contract_rows(): lax.dot_general(left_rows, right_rows, (((0,), (0,)), ((), ())), preferre...  21.7 us
    mul x2, other arithmetic, conv_module(): conv_kernel[tap_index] * padded[:, tap_index:tap_index + utt_len]  21.6 us
    dot_general x2, matrix products, times_transpose(): lax.dot_general(left_rows, matrix, (((1,), (1,)), ((), ())), preferred_el...  20.4 us
  transfers between devices with their start and end apart: 12, of which 8 were waited for; matrix products, arithmetic and copies ran while one was open for 47% of the time, Pallas kernels for 0%

profile of v5, /device:TPU:1, one launch (start us, length us, event | category | flops | bytes accessed | tf_op | source)
XLA Modules:
  0.0 333.4 jit_solution(11896533760743776361)
XLA Ops:
  8.6 1.1 reduce-window.6
  10.8 2.4 scatter_custom_fusion
  13.4 1.4 broadcast_select_fusion.2
  14.8 3.4 %gather_fusion = bf16[576,1024]{1,0:T(8,128)(2,1)} fusion(bf16[512,1024]{1,0:T(8,128)(2,1)S(1)} %broadcast_select_fusion.2, s32[1024]{0:T(1024)S(1)} %pad_clamp_fusion.1), kind=kCustom, calls=%fused_computation | custom fusion | bytes 2361600 | tf_op jit(solution)/shard_map/gather | solution.py:81
  18.2 2.6 broadcast_select_fusion.1
  20.8 6.9 %all-to-all-start = ((bf16[8,72,1024]{2,1,0:T(8,128)(2,1)}), bf16[8,72,1024]{2,1,0:T(8,128)(2,1)}, u32[]{:S(2)}, u32[]{:S(2)}) async-start(bf16[8,72,1024]{2,1,0:T(8,128)(2,1)} %broadcast_select_fusion.1), calls=%async_computation | async-start | bytes 2359296 | tf_op jit(solution)/shard_map/all_to_all | solution.py:82
  29.0 9.6 %multiply_add_fusion = (f32[2,256,1024]{2,1,0:T(8,128)S(1)}, f32[2,256,1024]{2,1,0:T(8,128)}) fusion(f32[2,256]{1,0:T(2,128)S(1)} %get-tuple-element.133, bf16[512,1024]{1,0:T(8,128)(2,1)S(1)} %copy-done, f32[1024]{0:T(1024)S(1)} %bitcast.205, f32[1024]{0:T(1024)S(1)} %bitcast.159, f32[1024]{0:T(1024)S(1)} %bitcast.161, f32[1024]{0:T(1024)S(1)} %bitcast.163, ...), kind=kLoop, calls=%fused_computation.105 | loop fusion | flops 35651584 | bytes 7469056 | tf_op jit(solution)/shard_map/add | solution.py:23
  39.6 3.4 %gather_fusion.1 = bf16[576,1024]{1,0:T(8,128)(2,1)} fusion(bf16[512,1024]{1,0:T(8,128)(2,1)S(1)} %bitcast.143, s32[1024]{0:T(1024)S(1)} %pad_clamp_fusion.1), kind=kCustom, calls=%fused_computation.1 | custom fusion | bytes 2361600 | tf_op jit(solution)/shard_map/gather | solution.py:92
  43.0 2.4 broadcast_select_fusion
  45.4 21.8 %all_to_all.20 = bf16[8,72,1024]{2,1,0:T(8,128)(2,1)S(1)} all-to-all(bf16[8,72,1024]{2,1,0:T(8,128)(2,1)} %bitcast.151), channel_id=1, replica_groups=mesh['dp'=16,'expert'=8] {'expert'}, dimensions={0} | all-to-all | bytes 2359296 | tf_op jit(solution)/shard_map/all_to_all | solution.py:94
  67.2 11.1 %multiply_convert_fusion.1 = (bf16[576,4096]{1,0:T(8,128)(2,1)S(1)}, f32[576,4096]{1,0:T(8,128)}) fusion(bf16[576,1024]{1,0:T(8,128)(2,1)S(1)} %bitcast.148, bf16[1,1024,4096]{2,1,0:T(8,128)(2,1)} %param.15), kind=kOutput, calls=%fused_computation.6 | convolution fusion | flops 4843634688 | bytes 23724032 | tf_op jit(solution)/shard_map/dot_general | solution.py:105
  78.4 2.2 copy-done.15
  80.6 11.5 %fusion.39 = f32[4096,1024]{1,0:T(8,128)} fusion(bf16[576,4096]{1,0:T(8,128)(2,1)S(1)} %get-tuple-element.21, bf16[576,1024]{1,0:T(8,128)(2,1)} %bitcast.44), kind=kOutput, calls=%fused_computation.181 | convolution fusion | flops 4831838208 | bytes 22675456 | tf_op jit(solution)/shard_map/dot_general | solution.py:33
  92.3 10.5 %multiply_convert_fusion = bf16[576,4096]{1,0:T(8,128)(2,1)S(1)} fusion(f32[576,4096]{1,0:T(8,128)} %get-tuple-element.20, bf16[576,1024]{1,0:T(8,128)(2,1)} %bitcast.44, bf16[1,4096,1024]{2,1,0:T(8,128)(2,1)} %param.16), kind=kOutput, calls=%fused_computation.5 | convolution fusion | flops 4853071872 | bytes 23724032 | tf_op jit(solution)/shard_map/dot_general | solution.py:39
  102.9 2.1 copy-done.7
  105.0 10.2 %fusion.40 = f32[1024,4096]{1,0:T(8,128)} fusion(bf16[576,1024]{1,0:T(8,128)(2,1)S(1)} %bitcast.149, bf16[576,4096]{1,0:T(8,128)(2,1)S(1)} %multiply_convert_fusion), kind=kOutput, calls=%fused_computation.182 | convolution fusion | flops 4831838208 | bytes 22675456 | tf_op jit(solution)/shard_map/dot_general | solution.py:33
  115.2 9.9 %fusion.24 = bf16[576,1024]{1,0:T(8,128)(2,1)} fusion(bf16[576,4096]{1,0:T(8,128)(2,1)} %copy-done.15, bf16[1,4096,1024]{2,1,0:T(8,128)(2,1)} %param.16), kind=kOutput, calls=%fused_computation.111 | convolution fusion | flops 4832428032 | bytes 14286848 | tf_op jit(solution)/shard_map/dot_general | solution.py:112
  125.1 9.9 %fusion.21 = bf16[576,1024]{1,0:T(8,128)(2,1)} fusion(bf16[576,4096]{1,0:T(8,128)(2,1)} %copy-done.7, bf16[1,1024,4096]{2,1,0:T(8,128)(2,1)} %param.15), kind=kOutput, calls=%fused_computation.110 | convolution fusion | flops 4832428032 | bytes 14286848 | tf_op jit(solution)/shard_map/dot_general | solution.py:39
  135.0 4.5 %all-to-all-start.3 = ((bf16[8,72,1024]{2,1,0:T(8,128)(2,1)}), bf16[8,72,1024]{2,1,0:T(8,128)(2,1)S(1)}, u32[]{:S(2)}, u32[]{:S(2)}) async-start(bf16[8,72,1024]{2,1,0:T(8,128)(2,1)} %bitcast.153), calls=%async_computation.3 | async-start | bytes 2359296 | tf_op jit(solution)/shard_map/all_to_all | solution.py:127
  139.6 16.3 %all-to-all-done.3 = bf16[8,72,1024]{2,1,0:T(8,128)(2,1)S(1)} async-done(((bf16[8,72,1024]{2,1,0:T(8,128)(2,1)}), bf16[8,72,1024]{2,1,0:T(8,128)(2,1)S(1)}, u32[]{:S(2)}, u32[]{:S(2)}) %all-to-all-start.3) | async-done | bytes 1179680 | tf_op jit(solution)/shard_map/all_to_all | solution.py:127
  155.9 2.8 gather_fusion.3
  158.7 2.7 fusion.16
  161.5 2.0 add_add_fusion.1
  163.4 1.9 reduce_sum.384
  165.3 20.3 %multiply_reduce_fusion.30 = (f32[1024]{0:T(1024)S(1)}, f32[1024]{0:T(1024)S(1)}, f32[1024]{0:T(1024)S(1)}, f32[1024]{0:T(1024)S(1)}, f32[1024]{0:T(1024)S(1)}, ...) fusion(f32[2,256,1024]{2,1,0:T(8,128)} %copy-done.4, ...), kind=kLoop, calls=%fused_computation.99 | loop fusion | flops 27249664 | bytes 11610624 | tf_op jit(solution)/shard_map/transpose(jvp())/reduce_sum | solution.py:22
  185.6 4.9 %multiply_reduce_fusion.31 = (f32[1024]{0:T(1024)S(1)}, f32[1024]{0:T(1024)S(1)}, f32[1024]{0:T(1024)S(1)}, f32[1024]{0:T(1024)S(1)}, f32[1024]{0:T(1024)S(1)}, ...) fusion(f32[2,256,1024]{2,1,0:T(8,128)S(1)} %get-tuple-element.6, ...), kind=kLoop, calls=%fused_computation.100 | loop fusion | flops 18855936 | bytes 4268032 | tf_op jit(solution)/shard_map/transpose(jvp())/reduce_sum | solution.py:22
  190.8 9.2 %broadcast_multiply_fusion.1 = (f32[2,256,1024]{2,1,0:T(8,128)}, f32[2,256,1024]{2,1,0:T(8,128)}, f32[2,256,1024]{2,1,0:T(8,128)}, f32[2,256,1024]{2,1,0:T(8,128...) fusion(f32[2,256,1024]{2,1,0:T(8,128)S(1)} %get-tuple-element.6, ...), kind=kLoop, calls=%fused_computation.115 | loop fusion | flops 6815744 | bytes 29413376 | tf_op jit(solution)/shard_map/transpose(jvp())/mul | solution.py:22
  200.0 12.4 %broadcast_multiply_fusion = (f32[2,256,1024]{2,1,0:T(8,128)}, f32[2,256,1024]{2,1,0:T(8,128)}, f32[2,256,1024]{2,1,0:T(8,128)}, f32[2,256,1024]{2,1,0:T(8,128)}...) fusion(f32[2,256,1024]{2,1,0:T(8,128)S(1)} %get-tuple-element.6, ...), kind=kLoop, calls=%fused_computation.114 | loop fusion | flops 9437184 | bytes 39919616 | tf_op jit(solution)/shard_map/transpose(jvp())/mul | solution.py:22
  212.4 22.7 %pad_add_fusion = f32[2,286,1024]{2,1,0:T(8,128)} fusion(f32[2,256,1024]{2,1,0:T(8,128)} %get-tuple-element.76, f32[2,256,1024]{2,1,0:T(8,128)} %get-tuple-element.77, f32[2,256,1024]{2,1,0:T(8,128)} %get-tuple-element.78, f32[2,256,1024]{2,1,0:T(8,128)} %get-tuple-element.79, f32[2,256,1024]{2,1,0:T(8,128)} %get-tuple-element.80, ...), kind=kLoop, calls=%fused_computation.18 | loop fusion | flops 14057472 | bytes 54771712 | tf_op jit(solution)/shard_map/transpose(jvp())/add_any | solution.py:22
  235.1 6.8 %multiply_reduce_fusion.32 = (f32[2,256]{1,0:T(2,128)S(1)}, f32[2,256,1024]{2,1,0:T(8,128)S(1)}, f32[2,256,1024]{2,1,0:T(8,128)S(1)}) fusion(f32[1024]{0:T(1024)S(1)} %copy-done.9, f32[2,256]{1,0:T(2,128)S(1)} %div.56, bf16[2,256,1024]{2,1,0:T(8,128)(2,1)S(1)} %bitcast.146, f32[2,256]{1,0:T(2,128)S(1)} %get-tuple-element.133, ...), kind=kLoop, calls=%fused_computation.102 | loop fusion | flops 6290944 | bytes 19933184 | tf_op jit(solution)/shard_map/transpose(jvp())/reduce_sum | solution.py:11
  241.9 1.1 multiply_reduce_fusion
  243.2 1.3 collective-permute-start
  244.5 1.0 collective-permute-done
  245.9 5.2 %collective-permute-done.1 = f32[33,1024]{1,0:T(8,128)S(1)} collective-permute-done((f32[33,1024]{1,0:T(8,128)S(1)}, f32[33,1024]{1,0:T(8,128)S(1)}, u32[]{:S(2)}, u32[]{:S(2)}) %collective-permute-start.1) | collective-permute-done | bytes 135200 | tf_op jit(solution)/shard_map/ppermute | solution.py:50
  251.1 1.0 collective-permute-start.2
  252.1 5.0 %all-to-all-start.2 = ((bf16[8,72,1024]{2,1,0:T(8,128)(2,1)}), bf16[8,72,1024]{2,1,0:T(8,128)(2,1)S(1)}, u32[]{:S(2)}, u32[]{:S(2)}) async-start(bf16[8,72,1024]{2,1,0:T(8,128)(2,1)} %bitcast.152), calls=%async_computation.2 | async-start | bytes 2359296 | tf_op jit(solution)/shard_map/all_to_all | solution.py:120
  257.4 1.0 add.385
  258.4 1.3 collective-permute-start.3
  259.7 7.6 %collective-permute-done.3 = f32[33,1024]{1,0:T(8,128)S(1)} collective-permute-done((f32[33,1024]{1,0:T(8,128)S(1)}, f32[33,1024]{1,0:T(8,128)S(1)}, u32[]{:S(2)}, u32[]{:S(2)}) %collective-permute-start.3) | collective-permute-done | bytes 135200 | tf_op jit(solution)/shard_map/ppermute | solution.py:50
  267.4 3.3 collective-permute-start.4
  270.7 7.4 %collective-permute-done.4 = f32[33,1024]{1,0:T(8,128)S(1)} collective-permute-done((f32[33,1024]{1,0:T(8,128)S(1)}, f32[33,1024]{1,0:T(8,128)S(1)}, u32[]{:S(2)}, u32[]{:S(2)}) %collective-permute-start.4) | collective-permute-done | bytes 135200 | tf_op jit(solution)/shard_map/ppermute | solution.py:50
  278.1 1.3 collective-permute-start.5
  279.5 3.9 %add_convert_fusion = bf16[2,256,1024]{2,1,0:T(8,128)(2,1)} fusion(f32[2,256]{1,0:T(2,128)S(1)} %negate_multiply_fusion, f32[2,256]{1,0:T(2,128)S(1)} %negate_multiply_fusion.1, f32[2,256]{1,0:T(2,128)S(1)} %multiply_multiply_fusion.1, f32[2,256]{1,0:T(2,128)S(1)} %div.56, f32[2,256]{1,0:T(2,128)S(1)} %rsqrt.22, f32[2,256,1024]{2,1,0:T(8,128)} %copy-done.6, ...), kind=kLoop, calls=%fused_computation.101 | loop fusion | flops 11010048 | bytes 8413696 | tf_op jit(solution)/shard_map/convert_element_type | solution.py:165
  283.4 2.8 gather_fusion.2
  287.1 3.0 collective-permute-start.6
  290.1 2.8 fusion.18
  292.8 3.0 collective-permute-done.6
  297.1 29.0 %reduce-scatter.3.cloned.1.call-done = f32[1024,256]{1,0:T(8,128)} async-done(((f32[1024,4096]{1,0:T(8,128)}), f32[1024,256]{1,0:T(8,128)}) %reduce-scatter.3.cloned.1.call-update) | async-done | bytes 1048592 | tf_op jit(solution)/shard_map/reduce_scatter | solution.py:117
  (86 shorter events, 8.6 us)
Async XLA Ops:
  13.3 4.9 %copy-start.13 = (pred[512]{0:T(512)(128)(4,1)}, pred[512]{0:T(512)(128)(4,1)S(1)}, u32[]{:S(2)}) copy-start(pred[512]{0:T(512)(128)(4,1)S(1)} %gt.26) | copy-start | bytes 1540
  18.2 9.5 %copy-start = (bf16[512,1024]{1,0:T(8,128)(2,1)S(1)}, bf16[512,1024]{1,0:T(8,128)(2,1)}, u32[]{:S(2)}) copy-start(bf16[512,1024]{1,0:T(8,128)(2,1)} %param.9) | copy-start | bytes 3145732
  20.8 7.6 %copy-start.8 = (f32[31,1024]{1,0:T(8,128)S(1)}, f32[31,1024]{1,0:T(8,128)}, u32[]{:S(2)}) copy-start(f32[31,1024]{1,0:T(8,128)} %param.12) | copy-start | bytes 380932
  20.8 7.8 %copy-start.9 = (f32[1024]{0:T(1024)S(1)}, f32[1024]{0:T(1024)}, u32[]{:S(2)}) copy-start(f32[1024]{0:T(1024)} %param.13) | copy-start | bytes 12292
  20.8 24.6 %all-to-all-start = ((bf16[8,72,1024]{2,1,0:T(8,128)(2,1)}), bf16[8,72,1024]{2,1,0:T(8,128)(2,1)}, u32[]{:S(2)}, u32[]{:S(2)}) async-start(bf16[8,72,1024]{2,1,0:T(8,128)(2,1)} %broadcast_select_fusion.1), calls=%async_computation | async-start | bytes 2359296 | tf_op jit(solution)/shard_map/all_to_all | solution.py:82
  27.7 269.4 %reduce-scatter.5.cloned.1.call-start = ((), (), s32[]{:S(2)}) async-start(), calls=%async_computation.7 | async-start | bytes 17825792 | tf_op jit(solution)/shard_map/reduce_scatter | solution.py:111
  28.5 10.0 %copy-start.11 = (f32[2,256]{1,0:T(2,128)}, f32[2,256]{1,0:T(2,128)S(1)}, u32[]{:S(2)}) copy-start(f32[2,256]{1,0:T(2,128)S(1)} %add.341) | copy-start | bytes 6148
  29.0 9.6 %copy-start.4 = (f32[2,256,1024]{2,1,0:T(8,128)}, f32[2,256,1024]{2,1,0:T(8,128)S(1)}, u32[]{:S(2)}) copy-start(f32[2,256,1024]{2,1,0:T(8,128)S(1)} %multiply_multiply_fusion) | copy-start | bytes 6291460
  38.6 0.7 copy-start.10
  78.4 2.2 copy-start.15
  92.1 234.0 %reduce-scatter.3.cloned.1.call-start = ((), (), s32[]{:S(2)}) async-start(), calls=%async_computation.6 | async-start | bytes 17825792 | tf_op jit(solution)/shard_map/reduce_scatter | solution.py:117
  102.9 2.1 copy-start.7
  135.0 20.9 %all-to-all-start.3 = ((bf16[8,72,1024]{2,1,0:T(8,128)(2,1)}), bf16[8,72,1024]{2,1,0:T(8,128)(2,1)S(1)}, u32[]{:S(2)}, u32[]{:S(2)}) async-start(bf16[8,72,1024]{2,1,0:T(8,128)(2,1)} %bitcast.153), calls=%async_computation.3 | async-start | bytes 2359296 | tf_op jit(solution)/shard_map/all_to_all | solution.py:127
  158.7 2.7 copy-start.3
  163.4 1.9 copy-start.1
  165.3 20.3 %copy-start.5 = (f32[2,256,1024]{2,1,0:T(8,128)S(1)}, f32[2,256,1024]{2,1,0:T(8,128)}, u32[]{:S(2)}) copy-start(f32[2,256,1024]{2,1,0:T(8,128)} %copy-done.4) | copy-start | bytes 6291460
  235.0 6.8 %copy-start.12 = (f32[2,256]{1,0:T(2,128)S(1)}, f32[2,256]{1,0:T(2,128)}, u32[]{:S(2)}) copy-start(f32[2,256]{1,0:T(2,128)} %copy-done.11) | copy-start | bytes 6148
  241.9 1.3 copy-start.6
  243.2 2.3 collective-permute-start
  245.5 5.6 %collective-permute-start.1 = (f32[33,1024]{1,0:T(8,128)S(1)}, f32[33,1024]{1,0:T(8,128)S(1)}, u32[]{:S(2)}, u32[]{:S(2)}) collective-permute-start(f32[33,1024]{1,0:T(8,128)S(1)} %fusion.34), channel_id=1, source_target_pairs={{0,2},{1,3},{2,0},{3,1},{4,6},{5,7},{6,4},{7,5},{8,10},{9,11},{10,... | collective-permute-start | bytes 405512 | tf_op jit(solution)/shard_map/ppermute | solution.py:50
  251.1 6.3 %collective-permute-start.2 = (f32[33,1024]{1,0:T(8,128)S(1)}, f32[33,1024]{1,0:T(8,128)}, u32[]{:S(2)}, u32[]{:S(2)}) collective-permute-start(f32[33,1024]{1,0:T(8,128)S(1)} %add.384), channel_id=1, source_target_pairs={{0,4},{1,5},{2,6},{3,7},{4,0},{5,1},{6,2},{7,3},{8,12},{9,13},{10,... | collective-permute-start | bytes 405512 | tf_op jit(solution)/shard_map/ppermute | solution.py:50
  252.1 31.3 %all-to-all-start.2 = ((bf16[8,72,1024]{2,1,0:T(8,128)(2,1)}), bf16[8,72,1024]{2,1,0:T(8,128)(2,1)S(1)}, u32[]{:S(2)}, u32[]{:S(2)}) async-start(bf16[8,72,1024]{2,1,0:T(8,128)(2,1)} %bitcast.152), calls=%async_computation.2 | async-start | bytes 2359296 | tf_op jit(solution)/shard_map/all_to_all | solution.py:120
  257.1 22.3 %copy-start.2 = (bf16[512,1024]{1,0:T(8,128)(2,1)S(1)}, bf16[512,1024]{1,0:T(8,128)(2,1)}, u32[]{:S(2)}) copy-start(bf16[512,1024]{1,0:T(8,128)(2,1)} %param.9) | copy-start | bytes 3145732
  258.4 8.9 %collective-permute-start.3 = (f32[33,1024]{1,0:T(8,128)S(1)}, f32[33,1024]{1,0:T(8,128)S(1)}, u32[]{:S(2)}, u32[]{:S(2)}) collective-permute-start(f32[33,1024]{1,0:T(8,128)S(1)} %add.385), channel_id=1, source_target_pairs={{0,8},{8,0},{16,24},{24,16},{32,40},{40,32},{48,56},{56,48},{64,72... | collective-permute-start | bytes 405512 | tf_op jit(solution)/shard_map/ppermute | solution.py:50
  267.4 10.7 %collective-permute-start.4 = (f32[33,1024]{1,0:T(8,128)S(1)}, f32[33,1024]{1,0:T(8,128)S(1)}, u32[]{:S(2)}, u32[]{:S(2)}) collective-permute-start(f32[33,1024]{1,0:T(8,128)S(1)} %add.386), channel_id=1, source_target_pairs={{0,16},{8,24},{16,0},{24,8},{32,48},{40,56},{48,32},{56,40},{64,80... | collective-permute-start | bytes 405512 | tf_op jit(solution)/shard_map/ppermute | solution.py:50
  278.1 8.0 %collective-permute-start.5 = (f32[33,1024]{1,0:T(8,128)S(1)}, f32[33,1024]{1,0:T(8,128)}, u32[]{:S(2)}, u32[]{:S(2)}) collective-permute-start(f32[33,1024]{1,0:T(8,128)S(1)} %add.387), channel_id=1, source_target_pairs={{0,32},{8,40},{16,48},{24,56},{32,0},{40,8},{48,16},{56,24},{64,96... | collective-permute-start | bytes 405512 | tf_op jit(solution)/shard_map/ppermute | solution.py:50
  283.4 6.7 %copy-start.14 = (pred[512]{0:T(512)(128)(4,1)S(1)}, pred[512]{0:T(512)(128)(4,1)}, u32[]{:S(2)}) copy-start(pred[512]{0:T(512)(128)(4,1)} %copy-done.13) | copy-start | bytes 1540
  287.1 8.7 %collective-permute-start.6 = (f32[33,1024]{1,0:T(8,128)S(1)}, f32[33,1024]{1,0:T(8,128)S(1)}, u32[]{:S(2)}, u32[]{:S(2)}) collective-permute-start(f32[33,1024]{1,0:T(8,128)S(1)} %add.388), channel_id=1, source_target_pairs={{0,64},{8,72},{16,80},{24,88},{32,96},{40,104},{48,112},{56,120},{... | collective-permute-start | bytes 405512 | tf_op jit(solution)/shard_map/ppermute | solution.py:50
Sparse Core Ops, SparseCore 0:
  92.2 109.6 reduce-scatter.4
  205.9 120.2 reduce-scatter.2
